TPU v7x, 128 devices: a whole 4x4x4 slice. The times are simulated.
128 devices in a mesh: feat: 32 (over z, x_hi, y), ex: 4 (over x_lo, core).
Axes of the slice: x: 4 (x_hi: 2, x_lo: 2; x = x_hi * 2 + x_lo), y: 4, z: 4, core: 2. Of those that a mesh axis runs over, the one named last changes fastest.
Arguments:
- grads: bfloat16 [256, 4194304], P('ex', 'feat'), may hold values from -6 to 6
- sign_bits: int32 [4194304], P('feat'), may hold values from 0 to 1
- sample_offset: int32 [8192], replicated, may hold values from 0 to 511
- queries: bfloat16 [16384, 8192], P('ex', 'feat'), may hold values from -6 to 6
- panel_order: int32 [32], replicated, may hold values from 0 to 31, each once
Outputs:
- scores: float32 [256, 16384], P('ex', 'feat')
Inputs may be any that keep to these rules, and one draw needn't show every extreme that they name: sample_offset is below 512. panel_order is a permutation.
All inputs are finite; a program needn't handle non-finite values.
Results may differ from a plain program's by a relative error of at most 0.018.
Values may be sent and summed in bfloat16 or wider, within the bound.
No kernel may reach another device: no remote copies, remote signals or barrier semaphores. Data moves between devices by JAX's collectives and lax.ppermute only.
A program may use at most 192 MiB of HBM per device.

v0:
```python
import math

import jax
import jax.numpy as jnp
from jax import lax
from jax.sharding import PartitionSpec as P

HA = 256
HB = 512
PROJ = 8192


def parity_of(values, bits):
    total = jnp.zeros_like(values)
    for position in range(bits):
        total = total ^ values >> position & 1
    return total


def hadamard_table(order, scale, dtype):
    index = jnp.arange(order, dtype=jnp.int32)
    parity = parity_of(index[:, None] & index[None, :], order.bit_length() - 1)
    return ((1 - 2 * parity).astype(jnp.float32) * scale).astype(dtype)


def power_scale(order):
    return 0.5 ** ((order.bit_length() - 1) // 2)


def on_device(grads, sign_bits, sample_offset, queries, panel_order):
    shards = lax.axis_size("feat")
    examples, feat_dev = grads.shape
    proj_dev = PROJ // shards
    stride = feat_dev // proj_dev
    scale_b = power_scale(HB)
    scale_a = power_scale(HA)
    cross = power_scale(feat_dev * shards) / (scale_a * scale_b)
    signed = grads * (1 - 2 * sign_bits).astype(jnp.bfloat16)[None, :]
    table_b = hadamard_table(HB, scale_b, jnp.bfloat16)
    table_a = hadamard_table(HA, scale_a, jnp.float32)
    section_one = jnp.dot(
        signed.reshape(examples * HA, HB), table_b, preferred_element_type=jnp.float32
    )
    section_one = section_one.reshape(examples, HA, HB)
    local = jnp.einsum("eab,ca->ecb", section_one, table_a, precision=lax.Precision.HIGHEST)
    local = local.astype(jnp.bfloat16).reshape(examples, feat_dev)
    device_id = lax.axis_index("feat")
    block_width = feat_dev // shards
    per_block = block_width // stride
    moved = lax.all_to_all(
        local.reshape(examples, shards, block_width),
        "feat",
        split_axis=1,
        concat_axis=1,
        tiled=True,
    )
    moved = moved.reshape(examples, shards, per_block, stride)
    offsets = lax.dynamic_slice_in_dim(
        sample_offset.reshape(shards, shards, per_block), device_id, 1, 1
    )[:, 0, :]
    picker = (jnp.arange(stride, dtype=jnp.int32)[None, None, :] == offsets[:, :, None]).astype(
        jnp.bfloat16
    )
    picked = jnp.einsum("edjr,ojr->edoj", moved, picker, preferred_element_type=jnp.float32)
    full_table = hadamard_table(shards, 1.0, jnp.float32)
    mixed = jnp.einsum("od,edoj->eoj", full_table, picked, precision=lax.Precision.HIGHEST) * cross
    returned = lax.all_to_all(
        mixed.astype(jnp.bfloat16), "feat", split_axis=1, concat_axis=2, tiled=True
    )
    projected = returned.reshape(examples, proj_dev)
    panel_count = panel_order.shape[0]
    partial_value = lax.dot_general(
        projected,
        lax.all_gather(queries, "ex", axis=0, tiled=True),
        (((1,), (1,)), ((), ())),
        preferred_element_type=jnp.float32,
    )
    ordered = jnp.take(
        partial_value.reshape(examples, panel_count, -1), panel_order, axis=1
    ).reshape(examples, -1)
    summed_scores = lax.psum_scatter(ordered, "feat", scatter_dimension=1, tiled=True)
    return summed_scores * (1.0 / math.sqrt(PROJ))


def solution(mesh):
    in_specs = (P("ex", "feat"), P("feat"), P(), P("ex", "feat"), P())
    out_specs = P("ex", "feat")
    return jax.shard_map(
        on_device, mesh=mesh, in_specs=in_specs, out_specs=out_specs, check_vma=False
    )
```

profile of v0, /device:TPU:8, one launch (start us, length us, event | category | flops | bytes accessed | tf_op | source)
XLA Modules:
  0.0 695.0 jit_solution(5106998455068920460)
XLA Ops:
  6.5 1.1 subtract_convert_fusion
  7.6 8.5 %broadcast_multiply_fusion = bf16[64,131072]{1,0:T(8,128)(2,1)S(1)} fusion(bf16[64,131072]{1,0:T(8,128)(2,1)} %param.5, bf16[131072]{0:T(1024)(128)(2,1)S(1)} %subtract_convert_fusion), kind=kLoop, calls=%fused_computation.5 | loop fusion | flops 8388608 | bytes 33816576 | tf_op jit(solution)/shard_map/mul | solution.py:38
  16.2 8.7 %copy.28 = bf16[8,8,256,512]{3,2,1,0:T(8,128)(2,1)} copy(bf16[8,8,256,512]{3,1,2,0:T(8,128)(2,1)S(1)} %bitcast.58) | data formatting | bytes 33554432
  24.9 21.7 %fusion.9 = f32[64,256,512]{2,1,0:T(8,128)} fusion(bf16[64,256,512]{2,1,0:T(8,128)(2,1)} %bitcast.57), kind=kOutput, calls=%fused_computation.12 | convolution fusion | flops 8598323200 | bytes 50331648 | tf_op jit(solution)/shard_map/dot_general | solution.py:41
  46.6 37.5 %convert_bitcast_fusion = bf16[64,256,512]{2,1,0:T(8,128)(2,1)} fusion(f32[64,256,512]{2,1,0:T(8,128)} %fusion.9), kind=kOutput, calls=%fused_computation.4 | convolution fusion | flops 25780027392 | bytes 50331648 | tf_op jit(solution)/shard_map/eab,ca->ecb/dot_general | solution.py:45
  84.1 25.6 %reshape_reshape.3 = bf16[64,32,4096]{2,1,0:T(8,128)(2,1)} reshape(bf16[64,256,512]{2,1,0:T(8,128)(2,1)} %convert_bitcast_fusion) | data formatting | bytes 33554432 | tf_op jit(solution)/shard_map/reshape;reshape | solution.py:51
  109.7 18.5 %copy.12 = bf16[64,32,4096]{2,0,1:T(8,128)(2,1)} copy(bf16[64,32,4096]{2,1,0:T(8,128)(2,1)} %reshape_reshape.3) | data formatting | bytes 33554432 | tf_op jit(solution)/shard_map/reshape;reshape | solution.py:51
  128.3 0.0 copy-start
  128.3 11.2 %all-to-all-start = ((bf16[64,32,4096]{2,0,1:T(8,128)(2,1)}), bf16[64,32,4096]{2,0,1:T(8,128)(2,1)}, u32[]{:S(2)}, u32[]{:S(2)}) async-start(bf16[64,32,4096]{2,0,1:T(8,128)(2,1)} %copy.12), calls=%async_computation | async-start | bytes 33554432 | tf_op jit(solution)/shard_map/all_to_all | solution.py:50
  139.5 0.3 all-gather.2.cloned.1.call-start
  139.7 0.5 all-gather.2.cloned.1.call-update
  140.2 0.0 copy-done
  140.2 0.3 reshape.29
  140.5 0.1 copy.11
  140.6 0.0 copy-done.1
  140.7 0.1 broadcast_bitcast_fusion
  140.7 277.3 %all-to-all-done = bf16[64,32,4096]{2,0,1:T(8,128)(2,1)} async-done(((bf16[64,32,4096]{2,0,1:T(8,128)(2,1)}), bf16[64,32,4096]{2,0,1:T(8,128)(2,1)}, u32[]{:S(2)}, u32[]{:S(2)}) %all-to-all-start) | async-done | bytes 16777248 | tf_op jit(solution)/shard_map/all_to_all | solution.py:50
  418.1 15.5 %fusion.5 = f32[64,32,32,8]{0,2,1,3:T(8,128)} fusion(bf16[32,8,8,8,512]{4,3,2,1,0:T(8,128)(2,1)} %bitcast.20, s32[32,8]{0,1:T(8,128)S(1)} %bitcast.65), kind=kOutput, calls=%fused_computation.8 | convolution fusion | flops 537001984 | bytes 18875392 | tf_op jit(solution)/shard_map/edjr,ojr->edoj/dot_general | solution.py:64
  433.5 7.9 %fusion.3 = f32[32,1,64,8]{2,1,3,0:T(1,128)S(1)} fusion(f32[32,32,1,1]{1,2,3,0:T(1,128)S(1)} %bitcast.64, f32[64,32,32,8]{0,2,1,3:T(8,128)} %fusion.5), kind=kOutput, calls=%fused_computation.6 | convolution fusion | flops 6291456 | bytes 2166784 | tf_op jit(solution)/shard_map/od,edoj->eoj/dot_general | solution.py:66
  441.4 0.7 reshape.48
  442.2 33.8 %all-to-all-start.1 = ((bf16[32,2,256]{2,1,0:T(2,128)(2,1)}), bf16[32,2,256]{2,1,0:T(2,128)(2,1)S(1)}, u32[]{:S(2)}, u32[]{:S(2)}) async-start(bf16[32,2,256]{2,1,0:T(2,128)(2,1)} %reshape.48), calls=%async_computation.1 | async-start | bytes 65536 | tf_op jit(solution)/shard_map/all_to_all | solution.py:67
  476.0 0.3 reduce-scatter.2.cloned.1.call-start
  476.3 8.3 %all-to-all-done.1 = bf16[32,2,256]{2,1,0:T(2,128)(2,1)S(1)} async-done(((bf16[32,2,256]{2,1,0:T(2,128)(2,1)}), bf16[32,2,256]{2,1,0:T(2,128)(2,1)S(1)}, u32[]{:S(2)}, u32[]{:S(2)}) %all-to-all-start.1) | async-done | bytes 32800 | tf_op jit(solution)/shard_map/all_to_all | solution.py:67
  484.7 0.1 reshape.49
  484.8 0.0 all-gather.2.cloned.1.call-done
  484.8 8.0 %fusion.65 = f32[64,32,512]{2,0,1:T(8,128)} fusion(bf16[32,512,256]{2,1,0:T(8,128)(2,1)} %bitcast.61, bf16[32,8,64]{2,1,0:T(8,128)(2,1)S(1)} %reshape.49), kind=kOutput, calls=%fused_computation.69 | convolution fusion | flops 536870912 | bytes 12615680 | tf_op jit(solution)/shard_map/dot_general | solution.py:72
  492.8 5.0 gather_fusion
  497.8 2.8 copy.26
  500.6 2.3 broadcast_select_fusion
  502.9 0.0 reduce-scatter.2.cloned.1.call-update
  502.9 183.7 %reduce-scatter.2.cloned.1.call-done = f32[64,512]{1,0:T(8,128)} async-done(((f32[64,16384]{1,0:T(8,128)}), f32[64,512]{1,0:T(8,128)}) %reduce-scatter.2.cloned.1.call-update) | async-done | bytes 131088 | tf_op jit(solution)/shard_map/reduce_scatter | solution.py:81
  686.5 1.6 broadcast_multiply_fusion.1
  (8 shorter events, 0.1 us)
Async XLA Ops:
  128.3 11.9 %copy-start = (s32[8192]{0:T(1024)S(1)}, s32[8192]{0:T(1024)}, u32[]{:S(2)}) copy-start(s32[8192]{0:T(1024)} %param.7) | copy-start | bytes 98308
  128.3 12.4 %copy-start.1 = (s32[32]{0:T(128)S(1)}, s32[32]{0:T(128)}, u32[]{:S(2)}) copy-start(s32[32]{0:T(128)} %param.9) | copy-start | bytes 388
  128.3 289.8 %all-to-all-start = ((bf16[64,32,4096]{2,0,1:T(8,128)(2,1)}), bf16[64,32,4096]{2,0,1:T(8,128)(2,1)}, u32[]{:S(2)}, u32[]{:S(2)}) async-start(bf16[64,32,4096]{2,0,1:T(8,128)(2,1)} %copy.12), calls=%async_computation | async-start | bytes 33554432 | tf_op jit(solution)/shard_map/all_to_all | solution.py:50
  139.5 345.3 %all-gather.2.cloned.1.call-start = ((), (), s32[]{:S(2)}) async-start(), calls=%async_computation.3 | async-start | bytes 10485760 | tf_op jit(solution)/shard_map/all_gather | solution.py:74
  442.2 42.5 %all-to-all-start.1 = ((bf16[32,2,256]{2,1,0:T(2,128)(2,1)}), bf16[32,2,256]{2,1,0:T(2,128)(2,1)S(1)}, u32[]{:S(2)}, u32[]{:S(2)}) async-start(bf16[32,2,256]{2,1,0:T(2,128)(2,1)} %reshape.48), calls=%async_computation.1 | async-start | bytes 65536 | tf_op jit(solution)/shard_map/all_to_all | solution.py:67
  476.0 210.6 %reduce-scatter.2.cloned.1.call-start = ((), (), s32[]{:S(2)}) async-start(), calls=%async_computation.4 | async-start | bytes 4325376 | tf_op jit(solution)/shard_map/reduce_scatter | solution.py:81
Sparse Core Ops, SparseCore 0:
  141.9 150.9 all-gather.1
  503.0 183.4 reduce-scatter.1
where the time goes:
time: 703 us; the launch traced here: 695 us
  waiting for transfers between devices  470 us (67%)
  matrix products  90.5 us (13%)
  local copies, waits for them, and re-layouts  62 us (9%)
  starting transfers between devices  45.5 us (6%)
  other arithmetic  13.5 us (2%)
  between operations  13.5 us (2%)
    all_to_all x1, waiting for transfers between devices, on_device(): lax.all_to_all(local.reshape(examples, shards, block_width), 'feat', spli...  277 us
    reduce_scatter x1, waiting for transfers between devices, on_device(): lax.psum_scatter(ordered, 'feat', scatter_dimension=1, tiled=True)  184 us
    another operation x2, local copies, waits for them, and re-layouts, on_device(): local.reshape(examples, shards, block_width)  44.2 us
    dot_general x1, matrix products, on_device(): jnp.einsum('eab,ca->ecb', section_one, table_a, precision=lax.Precision.H...  37.5 us
    all_to_all x1, starting transfers between devices, on_device(): lax.all_to_all(mixed.astype(jnp.bfloat16), 'feat', split_axis=1, concat_a...  33.8 us
    dot_general x1, matrix products, on_device(): jnp.dot(signed.reshape(examples * HA, HB), table_b, preferred_element_typ...  21.7 us
    dot_general x1, matrix products, on_device(): jnp.einsum('edjr,ojr->edoj', moved, picker, preferred_element_type=jnp.fl...  15.5 us
  transfers between devices with their start and end apart: 4, of which 3 were waited for; matrix products, arithmetic and copies ran while one was open for 4% of the time, Pallas kernels for 0%

commit v1 on v0

v1 whole, which is shorter than its diff:
```python
import math

import jax
import jax.numpy as jnp
from jax import lax
from jax.sharding import PartitionSpec as P

HA = 256
HB = 512
PROJ = 8192


def parity_of(values, bits):
    total = jnp.zeros_like(values)
    for position in range(bits):
        total = total ^ values >> position & 1
    return total


def hadamard_table(order, scale, dtype):
    index = jnp.arange(order, dtype=jnp.int32)
    parity = parity_of(index[:, None] & index[None, :], order.bit_length() - 1)
    return ((1 - 2 * parity).astype(jnp.float32) * scale).astype(dtype)


def power_scale(order):
    return 0.5 ** ((order.bit_length() - 1) // 2)


def on_device(grads, sign_bits, sample_offset, queries, panel_order):
    shards = lax.axis_size("feat")
    examples, feat_dev = grads.shape
    proj_dev = PROJ // shards
    scale_b = power_scale(HB)
    scale_a = power_scale(HA)
    cross = power_scale(feat_dev * shards) / (scale_a * scale_b)
    device_id = lax.axis_index("feat")

    signed = grads * (1 - 2 * sign_bits).astype(jnp.bfloat16)[None, :]
    table_a = hadamard_table(HA, scale_a, jnp.bfloat16)
    turned = jnp.einsum(
        "ca,eab->ceb",
        table_a,
        signed.reshape(examples, HA, HB),
        preferred_element_type=jnp.float32,
    )
    table_b = hadamard_table(HB, scale_b, jnp.bfloat16)
    rows = jnp.take(table_b, sample_offset, axis=0).reshape(shards, proj_dev, HB)
    high = turned.astype(jnp.bfloat16)
    low = (turned - high.astype(jnp.float32)).astype(jnp.bfloat16)
    both = jnp.concatenate([high, low], axis=1)
    picked = lax.dot_general(
        both, rows, (((2,), (2,)), ((0,), (1,))), preferred_element_type=jnp.float32
    )
    picked = picked[:, :examples] + picked[:, examples:]
    local = picked.astype(jnp.bfloat16)
    full_table = hadamard_table(shards, 1.0, jnp.bfloat16)
    signs = lax.dynamic_slice_in_dim(full_table, device_id, 1, 1)[:, 0]
    outgoing = jnp.transpose(local, (1, 2, 0)) * signs[None, :, None]
    returned = lax.all_to_all(outgoing, "feat", split_axis=1, concat_axis=1, tiled=True)
    projected = (jnp.sum(returned.astype(jnp.float32), axis=1) * cross).astype(jnp.bfloat16)

    every = lax.all_gather(projected, "ex", axis=0, tiled=True)
    partial_value = lax.dot_general(
        every, queries, (((1,), (1,)), ((), ())), preferred_element_type=jnp.float32
    )
    mine = lax.all_to_all(partial_value, "ex", split_axis=0, concat_axis=1, tiled=True)
    panel_count = panel_order.shape[0]
    ordered = jnp.take(mine.reshape(examples, panel_count, -1), panel_order, axis=1)
    gathered = lax.all_to_all(ordered, "feat", split_axis=1, concat_axis=1, tiled=True)
    summed_scores = jnp.sum(gathered, axis=1)
    return summed_scores * (1.0 / math.sqrt(PROJ))


def solution(mesh):
    in_specs = (P("ex", "feat"), P("feat"), P(), P("ex", "feat"), P())
    out_specs = P("ex", "feat")
    return jax.shard_map(
        on_device, mesh=mesh, in_specs=in_specs, out_specs=out_specs, check_vma=False
    )
```

time: 703 us -> 320 us (0.46); the launches traced: 695 us -> 319 us
  waiting for transfers between devices: 470 us -> 48.1 us
  blocking collectives: 0 us -> 91.1 us
  starting transfers between devices: 45.5 us -> 4.85 us
  other arithmetic: 13.5 us -> 44.1 us
  matrix products: 90.5 us -> 61.1 us
  between operations: 13.5 us -> 0.12 us
  local copies, waits for them, and re-layouts: 62 us -> 69.8 us
    all_to_all x2 -> x1, waiting for transfers between devices: 286 us -> 48.1 us  [on_device(): lax.all_to_all(partial_value, 'ex', split_axis=0, concat_axis=1, tiled=True)]
    reduce_scatter x1 -> x0, waiting for transfers between devices: 184 us -> none  [on_device(): lax.psum_scatter(ordered, 'feat', scatter_dimension=1, tiled=True)]
    all_to_all x0 -> x2, blocking collectives: none -> 85.4 us  [the longest x1 56.8 us: on_device(): lax.all_to_all(ordered, 'feat', split_axis=1, concat_axis=1, tiled=True)]
    another operation x2 -> x0, local copies, waits for them, and re-layouts: 44.2 us -> none  [on_device(): local.reshape(examples, shards, block_width)]
    all_to_all x2 -> x1, starting transfers between devices: 45 us -> 4.85 us  [on_device(): lax.all_to_all(partial_value, 'ex', split_axis=0, concat_axis=1, tiled=True)]
    gather x2, local copies, waits for them, and re-layouts: 7.78 us -> 38.6 us  [the longest x1 33.7 us: on_device(): jnp.take(table_b, sample_offset, axis=0).reshape(shards, proj_dev, HB)]
    dot_general x5 -> x3, matrix products: 90.5 us -> 61.1 us  [the longest x1 38.9 us: on_device(): lax.dot_general(both, rows, (((2,), (2,)), ((0,), (1,))), preferred_eleme...]
    concatenate x0 -> x1, other arithmetic: none -> 23 us  [on_device(): both = jnp.concatenate([high, low], axis=1)]
  transfers between devices with their start and end apart: 4 -> 1, of which waited for: 3 -> 1; matrix products, arithmetic and copies ran while one was open for 4% -> 0% of each run, Pallas kernels for 0% -> 0%
where the time goes in v1:
time: 320 us; the launch traced here: 319 us
  blocking collectives  91.1 us (28%)
  local copies, waits for them, and re-layouts  69.8 us (22%)
  matrix products  61.1 us (19%)
  waiting for transfers between devices  48.1 us (15%)
  other arithmetic  44.1 us (14%)
  starting transfers between devices  4.85 us (2%)
    all_to_all x1, blocking collectives, on_device(): lax.all_to_all(ordered, 'feat', split_axis=1, concat_axis=1, tiled=True)  56.8 us
    all_to_all x1, waiting for transfers between devices, on_device(): lax.all_to_all(partial_value, 'ex', split_axis=0, concat_axis=1, tiled=True)  48.1 us
    dot_general x1, matrix products, on_device(): lax.dot_general(both, rows, (((2,), (2,)), ((0,), (1,))), preferred_eleme...  38.9 us
    gather x1, local copies, waits for them, and re-layouts, on_device(): jnp.take(table_b, sample_offset, axis=0).reshape(shards, proj_dev, HB)  33.7 us
    all_to_all x1, blocking collectives, on_device(): lax.all_to_all(outgoing, 'feat', split_axis=1, concat_axis=1, tiled=True)  28.7 us
    concatenate x1, other arithmetic, on_device(): both = jnp.concatenate([high, low], axis=1)  23 us
    dot_general x1, matrix products, on_device(): jnp.einsum('ca,eab->ceb', table_a, signed.reshape(examples, HA, HB), pref...  19.5 us
    reshape x2, local copies, waits for them, and re-layouts, on_device(): mine.reshape(examples, panel_count, -1)  12.6 us
  transfers between devices with their start and end apart: 1, of which 1 were waited for; matrix products, arithmetic and copies ran while one was open for 0% of the time, Pallas kernels for 0%

profile of v1, /device:TPU:8, one launch (start us, length us, event | category | flops | bytes accessed | tf_op | source)
XLA Modules:
  0.0 319.2 jit_solution(18159316311973729986)
XLA Ops:
  0.0 0.0 copy-start
  0.0 1.1 multiply_convert_fusion
  1.1 0.8 fusion.19
  1.9 0.8 compare_and_fusion
  2.7 1.1 subtract_convert_fusion.1
  3.8 8.5 %broadcast_multiply_fusion = bf16[64,131072]{1,0:T(8,128)(2,1)S(1)} fusion(bf16[64,131072]{1,0:T(8,128)(2,1)} %param.5, bf16[131072]{0:T(1024)(128)(2,1)S(1)} %subtract_convert_fusion.1), kind=kLoop, calls=%fused_computation.7 | loop fusion | flops 8388608 | bytes 33816576 | tf_op jit(solution)/shard_map/mul | solution.py:39
  12.3 8.8 %copy.37 = bf16[8,8,256,512]{3,2,1,0:T(8,128)(2,1)} copy(bf16[8,8,256,512]{3,1,2,0:T(8,128)(2,1)S(1)} %bitcast.20) | data formatting | bytes 33554432
  21.1 19.5 %subtract_convert_fusion = (bf16[256,64,512]{2,0,1:T(8,128)(2,1)}, bf16[256,64,512]{2,0,1:T(8,128)(2,1)}) fusion(bf16[64,256,512]{2,1,0:T(8,128)(2,1)} %bitcast.19), kind=kOutput, calls=%fused_computation.5 | convolution fusion | flops 4330422272 | bytes 50331648 | tf_op jit(solution)/shard_map/ca,eab->ceb/dot_general | solution.py:41
  40.6 0.1 copy.28
  40.8 23.0 %pad_maximum_fusion = bf16[256,128,512]{2,0,1:T(8,128)(2,1)} fusion(bf16[256,64,512]{2,0,1:T(8,128)(2,1)} %get-tuple-element.5, bf16[256,64,512]{2,0,1:T(8,128)(2,1)} %get-tuple-element.6), kind=kLoop, calls=%fused_computation.2 | loop fusion | flops 16777216 | bytes 67108864 | tf_op jit(solution)/shard_map/concatenate | solution.py:51
  63.7 33.7 %gather_fusion = bf16[8192,512]{1,0:T(8,128)(2,1)} fusion(bf16[512,512]{1,0:T(8,128)(2,1)S(1)} %multiply_convert_fusion, s32[8192]{0:T(1024)S(1)} %fusion.19), kind=kCustom, calls=%fused_computation | custom fusion | bytes 16809984 | tf_op jit(solution)/shard_map/jit(_take)/gather | solution.py:48
  97.4 38.9 %fusion = f32[256,128,32]{1,2,0:T(8,128)S(1)} fusion(bf16[256,128,512]{2,0,1:T(8,128)(2,1)} %pad_maximum_fusion, bf16[32,256,512]{2,1,0:T(8,128)(2,1)} %bitcast.22, pred[32,256]{0,1:T(8,128)(4,1)S(1)} %copy.28), kind=kOutput, calls=%fused_computation.3 | convolution fusion | flops 1077936128 | bytes 46145536 | tf_op jit(solution)/shard_map/dot_general | solution.py:52
  136.3 2.5 fusion.6
  138.8 2.8 copy.31
  141.6 28.7 %all_to_all.26 = bf16[64,32,256]{2,0,1:T(8,128)(2,1)S(1)} all-to-all(bf16[64,32,256]{2,0,1:T(8,128)(2,1)S(1)} %copy.31), channel_id=1, replica_groups=mesh['feat'=32,'ex'=4] {'feat'}, dimensions={1} | all-to-all | bytes 2097152 | tf_op jit(solution)/shard_map/all_to_all | solution.py:60
  170.3 0.0 copy-start.1
  170.3 0.2 convert_reduce_fusion
  170.5 5.6 %all_gather.3 = bf16[256,256]{1,0:T(8,128)(2,1)S(1)} all-gather(bf16[64,256]{1,0:T(8,128)(2,1)S(1)} %multiply_convert_fusion.2), channel_id=1, replica_groups=mesh['feat'=32,'ex'=4] {'ex'}, dimensions={0}, use_global_device_ids=true | all-gather | bytes 163840 | tf_op jit(solution)/shard_map/all_gather | solution.py:63
  176.1 0.0 copy-done
  176.1 2.7 fusion.34
  178.8 4.9 %all-to-all-start.1 = ((f32[4,64,4096]{2,1,0:T(8,128)}), f32[4,64,4096]{2,1,0:T(8,128)}, u32[]{:S(2)}, u32[]{:S(2)}) async-start(f32[4,64,4096]{2,1,0:T(8,128)} %bitcast.21), calls=%async_computation.1 | async-start | bytes 8388608 | tf_op jit(solution)/shard_map/all_to_all | solution.py:67
  183.7 0.0 copy-done.1
  183.7 48.1 %all-to-all-done.1 = f32[4,64,4096]{2,1,0:T(8,128)} async-done(((f32[4,64,4096]{2,1,0:T(8,128)}), f32[4,64,4096]{2,1,0:T(8,128)}, u32[]{:S(2)}, u32[]{:S(2)}) %all-to-all-start.1) | async-done | bytes 4194336 | tf_op jit(solution)/shard_map/all_to_all | solution.py:67
  231.9 6.8 %copy.34 = f32[64,4,4096]{2,1,0:T(4,128)} copy(f32[64,4,4096]{2,0,1:T(8,128)} %bitcast.5) | data formatting | bytes 8388608 | tf_op jit(solution)/shard_map/all_to_all | solution.py:67
  238.7 6.1 %reshape.30 = f32[64,32,512]{2,1,0:T(8,128)} reshape(f32[64,4,4096]{2,1,0:T(4,128)} %copy.34) | data formatting | bytes 8388608 | tf_op jit(solution)/shard_map/reshape | solution.py:69
  244.8 6.6 %copy.35 = f32[64,32,512]{2,0,1:T(8,128)} copy(f32[64,32,512]{2,1,0:T(8,128)} %reshape.30) | data formatting | bytes 8388608 | tf_op jit(solution)/shard_map/reshape | solution.py:69
  251.4 4.9 %gather_fusion.1 = f32[32,64,512]{2,1,0:T(8,128)} fusion(f32[64,32,512]{2,0,1:T(8,128)} %copy.35, s32[1024]{0:T(1024)S(1)} %pad_clamp_fusion), kind=kCustom, calls=%fused_computation.1 | custom fusion | bytes 8388736 | tf_op jit(solution)/shard_map/jit(_take)/gather | solution.py:69
  256.3 2.9 select_bitcast_fusion
  259.3 56.8 %all_to_all.27 = f32[64,32,512]{2,0,1:T(8,128)} all-to-all(f32[64,32,512]{2,0,1:T(8,128)S(1)} %select_bitcast_fusion), channel_id=1, replica_groups=mesh['feat'=32,'ex'=4] {'feat'}, dimensions={1} | all-to-all | bytes 8388608 | tf_op jit(solution)/shard_map/all_to_all | solution.py:70
  316.0 2.5 reduce_sum.19
  318.5 0.7 broadcast_multiply_fusion.1
  (8 shorter events, 0.1 us)
Async XLA Ops:
  0.0 176.1 %copy-start = (bf16[4096,256]{1,0:T(8,128)(2,1)S(1)}, bf16[4096,256]{1,0:T(8,128)(2,1)}, u32[]{:S(2)}) copy-start(bf16[4096,256]{1,0:T(8,128)(2,1)} %param.8) | copy-start | bytes 6291460
  170.3 13.4 %copy-start.1 = (s32[32]{0:T(128)S(1)}, s32[32]{0:T(128)}, u32[]{:S(2)}) copy-start(s32[32]{0:T(128)} %param.9) | copy-start | bytes 388
  178.8 53.1 %all-to-all-start.1 = ((f32[4,64,4096]{2,1,0:T(8,128)}), f32[4,64,4096]{2,1,0:T(8,128)}, u32[]{:S(2)}, u32[]{:S(2)}) async-start(f32[4,64,4096]{2,1,0:T(8,128)} %bitcast.21), calls=%async_computation.1 | async-start | bytes 8388608 | tf_op jit(solution)/shard_map/all_to_all | solution.py:67

commit v2 on v1

--- a/solution.py
+++ b/solution.py
@@ -23,6 +23,22 @@
     return ((1 - 2 * parity).astype(jnp.float32) * scale).astype(dtype)
 
 
+def hadamard_rows(index, order, scale):
+    column = jnp.arange(order, dtype=jnp.int32)
+    parity = parity_fold(index[..., None] & column, order.bit_length() - 1)
+    return ((1 - 2 * parity).astype(jnp.float32) * scale).astype(jnp.bfloat16)
+
+
+def parity_fold(values, bits):
+    shift = 1
+    while shift < bits:
+        shift *= 2
+    while shift >= 1:
+        values = values ^ (values >> shift)
+        shift //= 2
+    return values & 1
+
+
 def power_scale(order):
     return 0.5 ** ((order.bit_length() - 1) // 2)
 
@@ -44,8 +60,7 @@
         signed.reshape(examples, HA, HB),
         preferred_element_type=jnp.float32,
     )
-    table_b = hadamard_table(HB, scale_b, jnp.bfloat16)
-    rows = jnp.take(table_b, sample_offset, axis=0).reshape(shards, proj_dev, HB)
+    rows = hadamard_rows(sample_offset.reshape(shards, proj_dev), HB, scale_b)
     high = turned.astype(jnp.bfloat16)
     low = (turned - high.astype(jnp.float32)).astype(jnp.bfloat16)
     both = jnp.concatenate([high, low], axis=1)
@@ -64,11 +79,13 @@
     partial_value = lax.dot_general(
         every, queries, (((1,), (1,)), ((), ())), preferred_element_type=jnp.float32
     )
-    mine = lax.all_to_all(partial_value, "ex", split_axis=0, concat_axis=1, tiled=True)
+    mine = lax.all_to_all(
+        partial_value.astype(jnp.bfloat16), "ex", split_axis=0, concat_axis=1, tiled=True
+    )
     panel_count = panel_order.shape[0]
     ordered = jnp.take(mine.reshape(examples, panel_count, -1), panel_order, axis=1)
     gathered = lax.all_to_all(ordered, "feat", split_axis=1, concat_axis=1, tiled=True)
-    summed_scores = jnp.sum(gathered, axis=1)
+    summed_scores = jnp.sum(gathered.astype(jnp.float32), axis=1)
     return summed_scores * (1.0 / math.sqrt(PROJ))
 
 

time: 320 us -> 224 us (0.70)
  local copies, waits for them, and re-layouts: 69.8 us -> 28.3 us
  blocking collectives: 91.1 us -> 68.3 us
  waiting for transfers between devices: 48.1 us -> 25.7 us
  matrix products: 61.1 us -> 54.9 us
    gather x1 -> x0, local copies, waits for them, and re-layouts: 33.7 us -> none  [on_device(): jnp.take(table_b, sample_offset, axis=0).reshape(shards, proj_dev, HB)]
    all_to_all x1, blocking collectives: 56.8 us -> 34.2 us  [on_device(): lax.all_to_all(ordered, 'feat', split_axis=1, concat_axis=1, tiled=True)]
    all_to_all x1, waiting for transfers between devices: 48.1 us -> 25.7 us  [on_device(): lax.all_to_all(partial_value.astype(jnp.bfloat16), 'ex', split_axis=0, co...]
    dot_general x1, matrix products: 38.9 us -> 33.4 us  [on_device(): lax.dot_general(both, rows, (((2,), (2,)), ((0,), (1,))), preferred_eleme...]
    reshape x2, local copies, waits for them, and re-layouts: 12.6 us -> 8.49 us  [on_device(): mine.reshape(examples, panel_count, -1)]
    mul x2, other arithmetic: 2.52 us -> 5.98 us  [on_device(): outgoing = jnp.transpose(local, (1, 2, 0)) * signs[None, :, None]]
    unnamed x5 -> x7, local copies, waits for them, and re-layouts: 8.8 us -> 8.77 us
where the time goes in v2:
time: 224 us; the launch traced here: 223 us
  blocking collectives  68.3 us (30%)
  matrix products  54.9 us (25%)
  other arithmetic  41.7 us (19%)
  local copies, waits for them, and re-layouts  28.3 us (13%)
  waiting for transfers between devices  25.7 us (11%)
  starting transfers between devices  4.43 us (2%)
    all_to_all x1, blocking collectives, on_device(): lax.all_to_all(ordered, 'feat', split_axis=1, concat_axis=1, tiled=True)  34.2 us
    dot_general x1, matrix products, on_device(): lax.dot_general(both, rows, (((2,), (2,)), ((0,), (1,))), preferred_eleme...  33.4 us
    all_to_all x1, blocking collectives, on_device(): lax.all_to_all(outgoing, 'feat', split_axis=1, concat_axis=1, tiled=True)  28.7 us
    all_to_all x1, waiting for transfers between devices, on_device(): lax.all_to_all(partial_value.astype(jnp.bfloat16), 'ex', split_axis=0, co...  25.7 us
    concatenate x1, other arithmetic, on_device(): both = jnp.concatenate([high, low], axis=1)  23 us
    dot_general x1, matrix products, on_device(): jnp.einsum('ca,eab->ceb', table_a, signed.reshape(examples, HA, HB), pref...  19.4 us
    unnamed x7, local copies, waits for them, and re-layouts  8.77 us
    mul x1, other arithmetic, on_device(): signed = grads * (1 - 2 * sign_bits).astype(jnp.bfloat16)[None, :]  8.52 us
  transfers between devices with their start and end apart: 1, of which 1 were waited for; matrix products, arithmetic and copies ran while one was open for 0% of the time, Pallas kernels for 0%

profile of v2, /device:TPU:8, one launch (start us, length us, event | category | flops | bytes accessed | tf_op | source)
XLA Modules:
  0.0 223.4 jit_solution(1009439687130609036)
XLA Ops:
  0.0 0.0 copy-start
  0.0 1.2 subtract_convert_fusion.1
  1.3 8.5 %broadcast_multiply_fusion = bf16[64,131072]{1,0:T(8,128)(2,1)S(1)} fusion(bf16[64,131072]{1,0:T(8,128)(2,1)} %param.5, bf16[131072]{0:T(1024)(128)(2,1)S(1)} %subtract_convert_fusion.1), kind=kLoop, calls=%fused_computation.23 | loop fusion | flops 8388608 | bytes 33816576 | tf_op jit(solution)/shard_map/mul | solution.py:55
  9.8 8.8 %copy.32 = bf16[8,8,256,512]{3,2,1,0:T(8,128)(2,1)} copy(bf16[8,8,256,512]{3,1,2,0:T(8,128)(2,1)S(1)} %bitcast.19) | data formatting | bytes 33554432
  18.6 0.0 copy-start.1
  18.6 19.4 %subtract_convert_fusion = (bf16[256,64,512]{2,0,1:T(8,128)(2,1)}, bf16[256,64,512]{2,0,1:T(8,128)(2,1)}) fusion(bf16[64,256,512]{2,1,0:T(8,128)(2,1)} %bitcast.18), kind=kOutput, calls=%fused_computation.4 | convolution fusion | flops 4330422272 | bytes 50331648 | tf_op jit(solution)/shard_map/ca,eab->ceb/dot_general | solution.py:57
  38.0 0.0 copy-done.1
  38.0 0.1 copy.24
  38.1 23.0 %pad_maximum_fusion = bf16[256,128,512]{2,0,1:T(8,128)(2,1)} fusion(bf16[256,64,512]{2,0,1:T(8,128)(2,1)} %get-tuple-element.5, bf16[256,64,512]{2,0,1:T(8,128)(2,1)} %get-tuple-element.6), kind=kLoop, calls=%fused_computation.1 | loop fusion | flops 16777216 | bytes 67108864 | tf_op jit(solution)/shard_map/concatenate | solution.py:66
  61.1 33.4 %fusion = f32[256,128,32]{1,2,0:T(8,128)} fusion(bf16[256,128,512]{2,0,1:T(8,128)(2,1)} %pad_maximum_fusion, s32[32,256]{0,1:T(8,128)S(1)} %copy.24), kind=kOutput, calls=%fused_computation.2 | convolution fusion | flops 1145044992 | bytes 37781504 | tf_op jit(solution)/shard_map/dot_general | solution.py:67
  94.5 0.0 copy-start.2
  94.5 6.0 %fusion.18 = bf16[64,32,256]{0,1,2:T(8,128)(2,1)} fusion(f32[256,128,32]{1,2,0:T(8,128)} %fusion, bf16[32]{0:T(256)(128)(2,1)S(1)} %convert_bitcast_fusion), kind=kLoop, calls=%fused_computation.29 | loop fusion | flops 1572864 | bytes 5242944 | tf_op jit(solution)/shard_map/mul | solution.py:74
  100.5 2.8 %copy.26 = bf16[64,32,256]{2,0,1:T(8,128)(2,1)S(1)} copy(bf16[64,32,256]{0,1,2:T(8,128)(2,1)} %fusion.18) | data formatting | bytes 2097152 | tf_op jit(solution)/shard_map/mul | solution.py:74
  103.3 28.7 %all_to_all.26 = bf16[64,32,256]{2,0,1:T(8,128)(2,1)S(1)} all-to-all(bf16[64,32,256]{2,0,1:T(8,128)(2,1)S(1)} %copy.26), channel_id=1, replica_groups=mesh['feat'=32,'ex'=4] {'feat'}, dimensions={1} | all-to-all | bytes 2097152 | tf_op jit(solution)/shard_map/all_to_all | solution.py:75
  132.0 0.2 convert_reduce_fusion.1
  132.1 5.4 %all_gather.3 = bf16[256,256]{1,0:T(8,128)(2,1)S(1)} all-gather(bf16[64,256]{1,0:T(8,128)(2,1)S(1)} %multiply_convert_fusion.1), channel_id=1, replica_groups=mesh['feat'=32,'ex'=4] {'ex'}, dimensions={0}, use_global_device_ids=true | all-gather | bytes 163840 | tf_op jit(solution)/shard_map/all_gather | solution.py:78
  137.5 0.0 copy-done
  137.5 2.0 convolution_convert_fusion
  139.6 4.4 %all-to-all-start.1 = ((bf16[4,64,4096]{2,1,0:T(8,128)(2,1)}), bf16[4,64,4096]{2,1,0:T(8,128)(2,1)}, u32[]{:S(2)}, u32[]{:S(2)}) async-start(bf16[4,64,4096]{2,1,0:T(8,128)(2,1)} %bitcast.20), calls=%async_computation.1 | async-start | bytes 4194304 | tf_op jit(solution)/shard_map/all_to_all | solution.py:82
  144.0 0.0 copy-done.2
  144.1 25.7 %all-to-all-done.1 = bf16[4,64,4096]{2,1,0:T(8,128)(2,1)} async-done(((bf16[4,64,4096]{2,1,0:T(8,128)(2,1)}), bf16[4,64,4096]{2,1,0:T(8,128)(2,1)}, u32[]{:S(2)}, u32[]{:S(2)}) %all-to-all-start.1) | async-done | bytes 2097184 | tf_op jit(solution)/shard_map/all_to_all | solution.py:82
  169.8 4.5 %copy.29 = bf16[64,4,4096]{2,1,0:T(4,128)(2,1)} copy(bf16[64,4,4096]{2,0,1:T(8,128)(2,1)} %bitcast.4) | data formatting | bytes 4194304 | tf_op jit(solution)/shard_map/all_to_all | solution.py:82
  174.3 4.4 %reshape.19 = bf16[64,32,512]{2,1,0:T(8,128)(2,1)} reshape(bf16[64,4,4096]{2,1,0:T(4,128)(2,1)} %copy.29) | data formatting | bytes 4194304 | tf_op jit(solution)/shard_map/reshape | solution.py:86
  178.7 4.1 %copy.30 = bf16[64,32,512]{2,0,1:T(8,128)(2,1)} copy(bf16[64,32,512]{2,1,0:T(8,128)(2,1)} %reshape.19) | data formatting | bytes 4194304 | tf_op jit(solution)/shard_map/reshape | solution.py:86
  182.8 3.6 %gather_fusion = bf16[32,64,512]{2,1,0:T(8,128)(2,1)} fusion(bf16[64,32,512]{2,0,1:T(8,128)(2,1)} %copy.30, s32[1024]{0:T(1024)S(1)} %pad_clamp_fusion), kind=kCustom, calls=%fused_computation | custom fusion | bytes 4194432 | tf_op jit(solution)/shard_map/jit(_take)/gather | solution.py:86
  186.4 1.8 select_bitcast_fusion
  188.2 34.2 %all_to_all.27 = bf16[64,32,512]{2,0,1:T(8,128)(2,1)S(1)} all-to-all(bf16[64,32,512]{2,0,1:T(8,128)(2,1)S(1)} %select_bitcast_fusion), channel_id=1, replica_groups=mesh['feat'=32,'ex'=4] {'feat'}, dimensions={1} | all-to-all | bytes 4194304 | tf_op jit(solution)/shard_map/all_to_all | solution.py:87
  222.4 0.3 convert_reduce_fusion
  222.7 0.7 broadcast_multiply_fusion.1
  (8 shorter events, 0.1 us)
Async XLA Ops:
  0.0 137.5 %copy-start = (bf16[4096,256]{1,0:T(8,128)(2,1)S(1)}, bf16[4096,256]{1,0:T(8,128)(2,1)}, u32[]{:S(2)}) copy-start(bf16[4096,256]{1,0:T(8,128)(2,1)} %param.8) | copy-start | bytes 6291460
  18.6 19.4 %copy-start.1 = (s32[8192]{0:T(1024)S(1)}, s32[8192]{0:T(1024)}, u32[]{:S(2)}) copy-start(s32[8192]{0:T(1024)} %param.7) | copy-start | bytes 98308
  94.5 49.5 %copy-start.2 = (s32[32]{0:T(128)S(1)}, s32[32]{0:T(128)}, u32[]{:S(2)}) copy-start(s32[32]{0:T(128)} %param.9) | copy-start | bytes 388
  139.6 30.2 %all-to-all-start.1 = ((bf16[4,64,4096]{2,1,0:T(8,128)(2,1)}), bf16[4,64,4096]{2,1,0:T(8,128)(2,1)}, u32[]{:S(2)}, u32[]{:S(2)}) async-start(bf16[4,64,4096]{2,1,0:T(8,128)(2,1)} %bitcast.20), calls=%async_computation.1 | async-start | bytes 4194304 | tf_op jit(solution)/shard_map/all_to_all | solution.py:82

commit v3 on v2

--- a/solution.py
+++ b/solution.py
@@ -61,31 +61,37 @@
         preferred_element_type=jnp.float32,
     )
     rows = hadamard_rows(sample_offset.reshape(shards, proj_dev), HB, scale_b)
-    high = turned.astype(jnp.bfloat16)
-    low = (turned - high.astype(jnp.float32)).astype(jnp.bfloat16)
-    both = jnp.concatenate([high, low], axis=1)
     picked = lax.dot_general(
-        both, rows, (((2,), (2,)), ((0,), (1,))), preferred_element_type=jnp.float32
+        turned.astype(jnp.bfloat16),
+        rows,
+        (((2,), (2,)), ((0,), (1,))),
+        preferred_element_type=jnp.float32,
     )
-    picked = picked[:, :examples] + picked[:, examples:]
     local = picked.astype(jnp.bfloat16)
     full_table = hadamard_table(shards, 1.0, jnp.bfloat16)
     signs = lax.dynamic_slice_in_dim(full_table, device_id, 1, 1)[:, 0]
-    outgoing = jnp.transpose(local, (1, 2, 0)) * signs[None, :, None]
-    returned = lax.all_to_all(outgoing, "feat", split_axis=1, concat_axis=1, tiled=True)
-    projected = (jnp.sum(returned.astype(jnp.float32), axis=1) * cross).astype(jnp.bfloat16)
+    outgoing = jnp.transpose(local, (2, 1, 0)) * signs[:, None, None]
+    returned = lax.all_to_all(outgoing, "feat", split_axis=0, concat_axis=0, tiled=True)
+    projected = (jnp.sum(returned.astype(jnp.float32), axis=0) * cross).astype(jnp.bfloat16)
 
     every = lax.all_gather(projected, "ex", axis=0, tiled=True)
     partial_value = lax.dot_general(
         every, queries, (((1,), (1,)), ((), ())), preferred_element_type=jnp.float32
     )
+    ex_count = lax.axis_size("ex")
     mine = lax.all_to_all(
-        partial_value.astype(jnp.bfloat16), "ex", split_axis=0, concat_axis=1, tiled=True
+        partial_value.astype(jnp.bfloat16).reshape(ex_count, examples, -1),
+        "ex",
+        split_axis=0,
+        concat_axis=0,
+        tiled=True,
     )
     panel_count = panel_order.shape[0]
-    ordered = jnp.take(mine.reshape(examples, panel_count, -1), panel_order, axis=1)
-    gathered = lax.all_to_all(ordered, "feat", split_axis=1, concat_axis=1, tiled=True)
-    summed_scores = jnp.sum(gathered.astype(jnp.float32), axis=1)
+    per_row = panel_count // ex_count
+    mine = mine.reshape(ex_count, examples, per_row, -1)
+    ordered = mine[panel_order // per_row, :, panel_order % per_row, :]
+    gathered = lax.all_to_all(ordered, "feat", split_axis=0, concat_axis=0, tiled=True)
+    summed_scores = jnp.sum(gathered.astype(jnp.float32), axis=0)
     return summed_scores * (1.0 / math.sqrt(PROJ))
 
 

time: 224 us -> 165 us (0.74)
  other arithmetic: 41.7 us -> 10.9 us
  matrix products: 54.9 us -> 36.6 us
  local copies, waits for them, and re-layouts: 28.3 us -> 18.5 us
    concatenate x1, other arithmetic: 23 us -> 0.02 us  [on_device(): ordered = mine[panel_order // per_row, :, panel_order % per_row, :]]
    dot_general x1, matrix products: 33.4 us -> 20.6 us  [on_device(): lax.dot_general(turned.astype(jnp.bfloat16), rows, (((2,), (2,)), ((0,),...]
    mul x2 -> x1, other arithmetic: 5.98 us -> 0.02 us  [on_device(): outgoing = jnp.transpose(local, (2, 1, 0)) * signs[:, None, None]]
    dot_general x1, matrix products: 19.4 us -> 14 us  [on_device(): jnp.einsum('ca,eab->ceb', table_a, signed.reshape(examples, HA, HB), pref...]
    reshape x2 -> x1, local copies, waits for them, and re-layouts: 8.49 us -> 3.19 us  [on_device(): mine = mine.reshape(ex_count, examples, per_row, -1)]
    all_to_all x1 -> x0, local copies, waits for them, and re-layouts: 4.51 us -> none  [on_device(): lax.all_to_all(partial_value.astype(jnp.bfloat16), 'ex', split_axis=0, co...]
where the time goes in v3:
time: 165 us
  blocking collectives  68.5 us (42%)
  matrix products  36.6 us (22%)
  waiting for transfers between devices  25.7 us (16%)
  local copies, waits for them, and re-layouts  18.5 us (11%)
  other arithmetic  10.9 us (7%)
  starting transfers between devices  4.43 us (3%)
    all_to_all x1, blocking collectives, on_device(): lax.all_to_all(ordered, 'feat', split_axis=0, concat_axis=0, tiled=True)  34.4 us
    all_to_all x1, blocking collectives, on_device(): lax.all_to_all(outgoing, 'feat', split_axis=0, concat_axis=0, tiled=True)  28.7 us
    all_to_all x1, waiting for transfers between devices, on_device(): lax.all_to_all(partial_value.astype(jnp.bfloat16).reshape(ex_count, examp...  25.7 us
    dot_general x1, matrix products, on_device(): lax.dot_general(turned.astype(jnp.bfloat16), rows, (((2,), (2,)), ((0,),...  20.6 us
    dot_general x1, matrix products, on_device(): jnp.einsum('ca,eab->ceb', table_a, signed.reshape(examples, HA, HB), pref...  14 us
    unnamed x7, local copies, waits for them, and re-layouts  8.79 us
    mul x1, other arithmetic, on_device(): signed = grads * (1 - 2 * sign_bits).astype(jnp.bfloat16)[None, :]  8.52 us
    all_gather x1, blocking collectives, on_device(): every = lax.all_gather(projected, 'ex', axis=0, tiled=True)  5.42 us
  transfers between devices with their start and end apart: 1, of which 1 were waited for; matrix products, arithmetic and copies ran while one was open for 0% of the time, Pallas kernels for 0%

profile of v3, /device:TPU:8, one launch (start us, length us, event | category | flops | bytes accessed | tf_op | source)
XLA Modules:
  0.0 164.7 jit_solution(14633218631031963955)
XLA Ops:
  0.0 0.0 copy-start
  0.0 1.2 subtract_convert_fusion
  1.3 8.5 %broadcast_multiply_fusion = bf16[64,131072]{1,0:T(8,128)(2,1)S(1)} fusion(bf16[64,131072]{1,0:T(8,128)(2,1)} %param.5, bf16[131072]{0:T(1024)(128)(2,1)S(1)} %subtract_convert_fusion), kind=kLoop, calls=%fused_computation.22 | loop fusion | flops 8388608 | bytes 33816576 | tf_op jit(solution)/shard_map/mul | solution.py:55
  9.8 8.8 %copy.30 = bf16[8,8,256,512]{3,2,1,0:T(8,128)(2,1)} copy(bf16[8,8,256,512]{3,1,2,0:T(8,128)(2,1)S(1)} %bitcast.18) | data formatting | bytes 33554432
  18.6 0.0 copy-start.1
  18.6 14.0 %convolution_convert_fusion = bf16[256,64,512]{2,0,1:T(8,128)(2,1)} fusion(bf16[64,256,512]{2,1,0:T(8,128)(2,1)} %bitcast.17), kind=kOutput, calls=%fused_computation.14 | convolution fusion | flops 4305256448 | bytes 33554432 | tf_op jit(solution)/shard_map/ca,eab->ceb/dot_general | solution.py:57
  32.5 0.0 copy-done.1
  32.6 0.1 copy.22
  32.7 0.0 copy-start.2
  32.7 20.6 %multiply_bitcast_fusion = bf16[32,64,256]{1,0,2:T(8,128)(2,1)} fusion(s32[32,256]{0,1:T(8,128)S(1)} %copy.22, bf16[256,64,512]{2,0,1:T(8,128)(2,1)} %convolution_convert_fusion, bf16[32]{0:T(256)(128)(2,1)S(1)} %convert_bitcast_fusion), kind=kOutput, calls=%fused_computation.27 | convolution fusion | flops 609222656 | bytes 17858624 | tf_op jit(solution)/shard_map/dot_general | solution.py:64
  53.3 2.8 %copy.24 = bf16[32,64,256]{2,1,0:T(8,128)(2,1)S(1)} copy(bf16[32,64,256]{1,0,2:T(8,128)(2,1)} %multiply_bitcast_fusion) | data formatting | bytes 2097152 | tf_op jit(solution)/shard_map/mul | solution.py:73
  56.1 28.7 %all_to_all.15 = bf16[32,64,256]{2,1,0:T(8,128)(2,1)S(1)} all-to-all(bf16[32,64,256]{2,1,0:T(8,128)(2,1)S(1)} %copy.24), channel_id=1, replica_groups=mesh['feat'=32,'ex'=4] {'feat'}, dimensions={0} | all-to-all | bytes 2097152 | tf_op jit(solution)/shard_map/all_to_all | solution.py:74
  84.8 0.2 convert_reduce_fusion.1
  84.9 5.4 %all_gather.3 = bf16[256,256]{1,0:T(8,128)(2,1)S(1)} all-gather(bf16[64,256]{1,0:T(8,128)(2,1)S(1)} %multiply_convert_fusion.1), channel_id=1, replica_groups=mesh['feat'=32,'ex'=4] {'ex'}, dimensions={0}, use_global_device_ids=true | all-gather | bytes 163840 | tf_op jit(solution)/shard_map/all_gather | solution.py:77
  90.4 0.0 copy-done
  90.4 2.1 %convolution_convert_fusion.1 = bf16[256,4096]{1,0:T(8,128)(2,1)} fusion(bf16[256,256]{1,0:T(8,128)(2,1)S(1)} %all_gather.3, bf16[4096,256]{1,0:T(8,128)(2,1)S(1)} %copy-done), kind=kOutput, calls=%fused_computation.23 | convolution fusion | flops 537919488 | bytes 4325376 | tf_op jit(solution)/shard_map/dot_general | solution.py:78
  92.4 4.4 %all-to-all-start.1 = ((bf16[4,64,4096]{2,1,0:T(8,128)(2,1)}), bf16[4,64,4096]{2,1,0:T(8,128)(2,1)}, u32[]{:S(2)}, u32[]{:S(2)}) async-start(bf16[4,64,4096]{2,1,0:T(8,128)(2,1)} %bitcast.19), calls=%async_computation.1 | async-start | bytes 4194304 | tf_op jit(solution)/shard_map/all_to_all | solution.py:82
  96.8 0.0 copy-done.2
  96.9 25.7 %all-to-all-done.1 = bf16[4,64,4096]{2,1,0:T(8,128)(2,1)} async-done(((bf16[4,64,4096]{2,1,0:T(8,128)(2,1)}), bf16[4,64,4096]{2,1,0:T(8,128)(2,1)}, u32[]{:S(2)}, u32[]{:S(2)}) %all-to-all-start.1) | async-done | bytes 2097184 | tf_op jit(solution)/shard_map/all_to_all | solution.py:82
  122.6 3.2 %copy.36 = bf16[4,8,8,8,512]{4,3,1,2,0:T(8,128)(2,1)} copy(bf16[4,8,8,8,512]{4,3,2,1,0:T(8,128)(2,1)} %bitcast.4) | data formatting | bytes 4194304 | tf_op jit(solution)/shard_map/reshape | solution.py:91
  125.8 3.6 %gather_fusion = bf16[32,64,512]{2,1,0:T(8,128)(2,1)} fusion(bf16[4,64,8,512]{3,1,2,0:T(8,128)(2,1)} %bitcast.20, s32[32]{0:T(128)S(1)} %fusion.38), kind=kCustom, calls=%fused_computation | custom fusion | bytes 4194560 | tf_op jit(solution)/shard_map/gather | solution.py:92
  129.4 34.4 %all_to_all.16 = bf16[32,64,512]{2,1,0:T(8,128)(2,1)S(1)} all-to-all(bf16[32,64,512]{2,1,0:T(8,128)(2,1)} %gather_fusion), channel_id=1, replica_groups=mesh['feat'=32,'ex'=4] {'feat'}, dimensions={0} | all-to-all | bytes 4194304 | tf_op jit(solution)/shard_map/all_to_all | solution.py:93
  163.8 0.3 convert_reduce_fusion
  164.1 0.7 broadcast_multiply_fusion.1
  (6 shorter events, 0.1 us)
Async XLA Ops:
  0.0 90.4 %copy-start = (bf16[4096,256]{1,0:T(8,128)(2,1)S(1)}, bf16[4096,256]{1,0:T(8,128)(2,1)}, u32[]{:S(2)}) copy-start(bf16[4096,256]{1,0:T(8,128)(2,1)} %param.8) | copy-start | bytes 6291460
  18.6 14.0 %copy-start.1 = (s32[8192]{0:T(1024)S(1)}, s32[8192]{0:T(1024)}, u32[]{:S(2)}) copy-start(s32[8192]{0:T(1024)} %param.7) | copy-start | bytes 98308
  32.7 64.2 %copy-start.2 = (s32[32]{0:T(128)S(1)}, s32[32]{0:T(128)}, u32[]{:S(2)}) copy-start(s32[32]{0:T(128)} %param.9) | copy-start | bytes 388
  92.4 30.2 %all-to-all-start.1 = ((bf16[4,64,4096]{2,1,0:T(8,128)(2,1)}), bf16[4,64,4096]{2,1,0:T(8,128)(2,1)}, u32[]{:S(2)}, u32[]{:S(2)}) async-start(bf16[4,64,4096]{2,1,0:T(8,128)(2,1)} %bitcast.19), calls=%async_computation.1 | async-start | bytes 4194304 | tf_op jit(solution)/shard_map/all_to_all | solution.py:82

commit v4 on v2

v4 whole, which is shorter than its diff:
```python
import math

import jax
import jax.numpy as jnp
from jax import lax
from jax.sharding import PartitionSpec as P

HA = 256
HB = 512
PROJ = 8192


def parity_of(values, bits):
    total = jnp.zeros_like(values)
    for position in range(bits):
        total = total ^ values >> position & 1
    return total


def hadamard_table(order, scale, dtype):
    index = jnp.arange(order, dtype=jnp.int32)
    parity = parity_of(index[:, None] & index[None, :], order.bit_length() - 1)
    return ((1 - 2 * parity).astype(jnp.float32) * scale).astype(dtype)


def hadamard_rows(index, order, scale):
    column = jnp.arange(order, dtype=jnp.int32)
    parity = parity_fold(index[..., None] & column, order.bit_length() - 1)
    return ((1 - 2 * parity).astype(jnp.float32) * scale).astype(jnp.bfloat16)


def parity_fold(values, bits):
    shift = 1
    while shift < bits:
        shift *= 2
    while shift >= 1:
        values = values ^ (values >> shift)
        shift //= 2
    return values & 1


def power_scale(order):
    return 0.5 ** ((order.bit_length() - 1) // 2)


def on_device(grads, sign_bits, sample_offset, queries, panel_order):
    shards = lax.axis_size("feat")
    examples, feat_dev = grads.shape
    proj_dev = PROJ // shards
    scale_b = power_scale(HB)
    scale_a = power_scale(HA)
    cross = power_scale(feat_dev * shards) / (scale_a * scale_b)
    device_id = lax.axis_index("feat")

    table_a = hadamard_table(HA, scale_a, jnp.bfloat16)
    flips = (1 - 2 * sign_bits).astype(jnp.bfloat16)[None, :]
    rows = hadamard_rows(sample_offset.reshape(shards, proj_dev), HB, scale_b)
    full_table = hadamard_table(shards, 1.0, jnp.bfloat16)
    signs = lax.dynamic_slice_in_dim(full_table, device_id, 1, 1)[:, 0]

    def local_part(block):
        signed = (block * flips).reshape(block.shape[0], HA, HB)
        turned = jnp.einsum("ca,eab->ceb", table_a, signed, preferred_element_type=jnp.float32)
        picked = lax.dot_general(
            turned.astype(jnp.bfloat16),
            rows,
            (((2,), (2,)), ((0,), (1,))),
            preferred_element_type=jnp.float32,
        )
        return jnp.transpose(picked.astype(jnp.bfloat16), (2, 1, 0)) * signs[:, None, None]

    ex_count = lax.axis_size("ex")
    panel_count = panel_order.shape[0]
    per_row = panel_count // ex_count
    halves = 2
    part = examples // halves
    in_flight = []
    for half in range(halves):
        piece = local_part(grads[half * part : (half + 1) * part])
        returned = lax.all_to_all(piece, "feat", split_axis=0, concat_axis=0, tiled=True)
        projected = (jnp.sum(returned.astype(jnp.float32), axis=0) * cross).astype(jnp.bfloat16)
        every = lax.all_gather(projected, "ex", axis=0, tiled=True)
        partial_value = lax.dot_general(
            every, queries, (((1,), (1,)), ((), ())), preferred_element_type=jnp.float32
        )
        in_flight.append(
            lax.all_to_all(
                partial_value.astype(jnp.bfloat16).reshape(ex_count, part, -1),
                "ex",
                split_axis=0,
                concat_axis=0,
                tiled=True,
            )
        )
    sums = []
    for mine in in_flight:
        mine = mine.reshape(ex_count, part, per_row, -1)
        ordered = mine[panel_order // per_row, :, panel_order % per_row, :]
        gathered = lax.all_to_all(ordered, "feat", split_axis=0, concat_axis=0, tiled=True)
        sums.append(jnp.sum(gathered.astype(jnp.float32), axis=0))
    summed_scores = jnp.concatenate(sums, axis=0)
    return summed_scores * (1.0 / math.sqrt(PROJ))


def solution(mesh):
    in_specs = (P("ex", "feat"), P("feat"), P(), P("ex", "feat"), P())
    out_specs = P("ex", "feat")
    return jax.shard_map(
        on_device, mesh=mesh, in_specs=in_specs, out_specs=out_specs, check_vma=False
    )
```

time: 224 us -> 216 us (0.964)
  blocking collectives: 68.3 us -> 21.4 us
  starting transfers between devices: 4.43 us -> 41.5 us
  other arithmetic: 41.7 us -> 16.6 us
  waiting for transfers between devices: 25.7 us -> 43.2 us
  local copies, waits for them, and re-layouts: 28.3 us -> 38.5 us
    all_to_all x2 -> x0, blocking collectives: 62.9 us -> none  [the longest x1 34.2 us: on_device(): lax.all_to_all(ordered, 'feat', split_axis=1, concat_axis=1, tiled=True)]
    all_to_all x1 -> x6, starting transfers between devices: 4.43 us -> 41.5 us  [the longest x2 20.8 us: on_device(): lax.all_to_all(piece, 'feat', split_axis=0, concat_axis=0, tiled=True)]
    concatenate x1, other arithmetic: 23 us -> 0.02 us  [on_device(): ordered = mine[panel_order // per_row, :, panel_order % per_row, :]]
    all_to_all x1 -> x6, waiting for transfers between devices: 25.7 us -> 43.2 us  [the longest x2 29.6 us: on_device(): lax.all_to_all(ordered, 'feat', split_axis=0, concat_axis=0, tiled=True)]
    all_gather x1 -> x2, blocking collectives: 5.42 us -> 21.4 us  [on_device(): every = lax.all_gather(projected, 'ex', axis=0, tiled=True)]
    unnamed x7 -> x10, local copies, waits for them, and re-layouts: 8.77 us -> 20.5 us
    mul x1 -> x2, local copies, waits for them, and re-layouts: 2.79 us -> 8.72 us  [local_part(): jnp.transpose(picked.astype(jnp.bfloat16), (2, 1, 0)) * signs[:, None, None]]
    reshape x2, local copies, waits for them, and re-layouts: 8.49 us -> 3.51 us  [on_device(): mine = mine.reshape(ex_count, part, per_row, -1)]
  transfers between devices with their start and end apart: 1 -> 6, of which waited for: 1 -> 4; matrix products, arithmetic and copies ran while one was open for 0% -> 25% of each run, Pallas kernels for 0% -> 0%
where the time goes in v4:
time: 216 us; the launch traced here: 215 us
  matrix products  53.5 us (25%)
  waiting for transfers between devices  43.2 us (20%)
  starting transfers between devices  41.5 us (19%)
  local copies, waits for them, and re-layouts  38.5 us (18%)
  blocking collectives  21.4 us (10%)
  other arithmetic  16.6 us (8%)
    dot_general x2, matrix products, local_part(): lax.dot_general(turned.astype(jnp.bfloat16), rows, (((2,), (2,)), ((0,),...  34.9 us
    all_to_all x2, waiting for transfers between devices, on_device(): lax.all_to_all(ordered, 'feat', split_axis=0, concat_axis=0, tiled=True)  29.6 us
    all_gather x2, blocking collectives, on_device(): every = lax.all_gather(projected, 'ex', axis=0, tiled=True)  21.4 us
    all_to_all x2, starting transfers between devices, on_device(): lax.all_to_all(piece, 'feat', split_axis=0, concat_axis=0, tiled=True)  20.8 us
    unnamed x10, local copies, waits for them, and re-layouts  20.5 us
    dot_general x2, matrix products, local_part(): jnp.einsum('ca,eab->ceb', table_a, signed, preferred_element_type=jnp.flo...  15 us
    all_to_all x2, starting transfers between devices, on_device(): lax.all_to_all(ordered, 'feat', split_axis=0, concat_axis=0, tiled=True)  12.9 us
    mul x1, other arithmetic, local_part(): signed = (block * flips).reshape(block.shape[0], HA, HB)  11.8 us
  transfers between devices with their start and end apart: 6, of which 4 were waited for; matrix products, arithmetic and copies ran while one was open for 25% of the time, Pallas kernels for 0%

profile of v4, /device:TPU:8, one launch (start us, length us, event | category | flops | bytes accessed | tf_op | source)
XLA Modules:
  0.0 214.8 jit_solution(14922256133295143690)
XLA Ops:
  0.0 1.2 subtract_convert_fusion
  1.3 11.8 %slice_multiply_fusion.1 = (bf16[32,131072]{1,0:T(8,128)(2,1)}, bf16[32,131072]{1,0:T(8,128)(2,1)}) fusion(bf16[64,131072]{1,0:T(8,128)(2,1)} %param.5, bf16[131072]{0:T(1024)(128)(2,1)S(1)} %subtract_convert_fusion), kind=kLoop, calls=%fused_computation.18 | loop fusion | flops 8388608 | bytes 33816576 | tf_op jit(solution)/shard_map/mul | solution.py:62
  13.1 9.8 %copy.50 = bf16[4,8,256,512]{3,2,1,0:T(8,128)(2,1)} copy(bf16[4,8,256,512]{3,1,2,0:T(8,128)(2,1)} %bitcast.33) | data formatting | bytes 16777216
  23.0 9.1 %convolution_convert_fusion.1 = bf16[256,32,512]{2,0,1:T(8,128)(2,1)} fusion(bf16[32,256,512]{2,1,0:T(8,128)(2,1)} %bitcast.30), kind=kOutput, calls=%fused_computation.20 | convolution fusion | flops 2153578496 | bytes 16777216 | tf_op jit(solution)/shard_map/ca,eab->ceb/dot_general | solution.py:63
  32.2 16.5 %multiply_bitcast_fusion.1 = bf16[32,32,256]{0,1,2:T(8,128)(2,1)} fusion(s32[32,256]{0,1:T(8,128)S(1)} %copy.35, bf16[256,32,512]{2,0,1:T(8,128)(2,1)} %convolution_convert_fusion.1, bf16[32]{0:T(256)(128)(2,1)S(1)} %convert_bitcast_fusion), kind=kOutput, calls=%fused_computation.26 | convolution fusion | flops 340262912 | bytes 8945728 | tf_op jit(solution)/shard_map/dot_general | solution.py:64
  48.7 4.4 %copy.37 = bf16[32,32,256]{2,1,0:T(8,128)(2,1)} copy(bf16[32,32,256]{0,1,2:T(8,128)(2,1)} %multiply_bitcast_fusion.1) | data formatting | bytes 1048576 | tf_op jit(solution)/shard_map/mul | solution.py:70
  53.1 11.0 %all-to-all-start = ((bf16[32,32,256]{2,1,0:T(8,128)(2,1)}), bf16[32,32,256]{2,1,0:T(8,128)(2,1)S(1)}, u32[]{:S(2)}, u32[]{:S(2)}) async-start(bf16[32,32,256]{2,1,0:T(8,128)(2,1)} %copy.37), calls=%async_computation | async-start | bytes 1048576 | tf_op jit(solution)/shard_map/all_to_all | solution.py:80
  64.1 9.8 %copy.51 = bf16[4,8,256,512]{3,2,1,0:T(8,128)(2,1)} copy(bf16[4,8,256,512]{3,1,2,0:T(8,128)(2,1)} %bitcast.32) | data formatting | bytes 16777216
  73.9 5.9 %convolution_convert_fusion = bf16[256,32,512]{2,0,1:T(8,128)(2,1)S(1)} fusion(bf16[32,256,512]{2,1,0:T(8,128)(2,1)} %bitcast.31), kind=kOutput, calls=%fused_computation.19 | convolution fusion | flops 2153578496 | bytes 16777216 | tf_op jit(solution)/shard_map/ca,eab->ceb/dot_general | solution.py:63
  79.8 18.4 %multiply_bitcast_fusion = bf16[32,32,256]{0,1,2:T(8,128)(2,1)} fusion(s32[32,256]{0,1:T(8,128)S(1)} %copy.35, bf16[256,32,512]{2,0,1:T(8,128)(2,1)S(1)} %convolution_convert_fusion, bf16[32]{0:T(256)(128)(2,1)S(1)} %convert_bitcast_fusion), kind=kOutput, calls=%fused_computation.24 | convolution fusion | flops 340262912 | bytes 8945728 | tf_op jit(solution)/shard_map/dot_general | solution.py:64
  98.2 4.4 %copy.42 = bf16[32,32,256]{2,1,0:T(8,128)(2,1)} copy(bf16[32,32,256]{0,1,2:T(8,128)(2,1)} %multiply_bitcast_fusion) | data formatting | bytes 1048576 | tf_op jit(solution)/shard_map/mul | solution.py:70
  102.6 9.8 %all-to-all-start.3 = ((bf16[32,32,256]{2,1,0:T(8,128)(2,1)}), bf16[32,32,256]{2,1,0:T(8,128)(2,1)S(1)}, u32[]{:S(2)}, u32[]{:S(2)}) async-start(bf16[32,32,256]{2,1,0:T(8,128)(2,1)} %copy.42), calls=%async_computation.3 | async-start | bytes 1048576 | tf_op jit(solution)/shard_map/all_to_all | solution.py:80
  112.5 6.9 %all_gather.6 = bf16[128,256]{1,0:T(8,128)(2,1)S(1)} all-gather(bf16[32,256]{1,0:T(8,128)(2,1)S(1)} %multiply_convert_fusion.2), channel_id=1, replica_groups=mesh['feat'=32,'ex'=4] {'ex'}, dimensions={0}, use_global_device_ids=true | all-gather | bytes 81920 | tf_op jit(solution)/shard_map/all_gather | solution.py:82
  119.4 1.8 convolution_convert_fusion.3
  121.2 3.1 %all-to-all-done.3 = bf16[32,32,256]{2,1,0:T(8,128)(2,1)S(1)} async-done(((bf16[32,32,256]{2,1,0:T(8,128)(2,1)}), bf16[32,32,256]{2,1,0:T(8,128)(2,1)S(1)}, u32[]{:S(2)}, u32[]{:S(2)}) %all-to-all-start.3) | async-done | bytes 524320 | tf_op jit(solution)/shard_map/all_to_all | solution.py:80
  124.3 0.8 copy-done.1
  125.1 3.5 %all-to-all-start.1 = ((bf16[4,32,4096]{2,1,0:T(8,128)(2,1)}), bf16[4,32,4096]{2,1,0:T(8,128)(2,1)S(1)}, u32[]{:S(2)}, u32[]{:S(2)}) async-start(bf16[4,32,4096]{2,1,0:T(8,128)(2,1)} %bitcast.3), calls=%async_computation.1 | async-start | bytes 2097152 | tf_op jit(solution)/shard_map/all_to_all | solution.py:87
  128.6 1.1 convert_reduce_fusion.2
  129.8 14.4 %all_gather.7 = bf16[128,256]{1,0:T(8,128)(2,1)S(1)} all-gather(bf16[32,256]{1,0:T(8,128)(2,1)S(1)} %multiply_convert_fusion.1), channel_id=1, replica_groups=mesh['feat'=32,'ex'=4] {'ex'}, dimensions={0}, use_global_device_ids=true | all-gather | bytes 81920 | tf_op jit(solution)/shard_map/all_gather | solution.py:82
  144.2 1.8 convolution_convert_fusion.2
  146.0 4.3 %all-to-all-start.4 = ((bf16[4,32,4096]{2,1,0:T(8,128)(2,1)}), bf16[4,32,4096]{2,1,0:T(8,128)(2,1)}, u32[]{:S(2)}, u32[]{:S(2)}) async-start(bf16[4,32,4096]{2,1,0:T(8,128)(2,1)} %bitcast.5), calls=%async_computation.4 | async-start | bytes 2097152 | tf_op jit(solution)/shard_map/all_to_all | solution.py:87
  150.3 1.1 copy.63
  151.5 2.8 %gather_fusion = bf16[32,32,512]{2,1,0:T(8,128)(2,1)} fusion(bf16[4,32,8,512]{3,1,2,0:T(8,128)(2,1)} %bitcast.36, s32[32]{0:T(128)S(1)} %fusion.37), kind=kCustom, calls=%fused_computation | custom fusion | bytes 2097408 | tf_op jit(solution)/shard_map/gather | solution.py:98
  154.3 10.5 %all-to-all-done.4 = bf16[4,32,4096]{2,1,0:T(8,128)(2,1)} async-done(((bf16[4,32,4096]{2,1,0:T(8,128)(2,1)}), bf16[4,32,4096]{2,1,0:T(8,128)(2,1)}, u32[]{:S(2)}, u32[]{:S(2)}) %all-to-all-start.4) | async-done | bytes 1048608 | tf_op jit(solution)/shard_map/all_to_all | solution.py:87
  164.8 7.3 %all-to-all-start.2 = ((bf16[32,32,512]{2,1,0:T(8,128)(2,1)}), bf16[32,32,512]{2,1,0:T(8,128)(2,1)S(1)}, u32[]{:S(2)}, u32[]{:S(2)}) async-start(bf16[32,32,512]{2,1,0:T(8,128)(2,1)} %gather_fusion), calls=%async_computation.2 | async-start | bytes 2097152 | tf_op jit(solution)/shard_map/all_to_all | solution.py:99
  172.1 2.4 %copy.62 = bf16[4,4,8,8,512]{4,3,1,2,0:T(8,128)(2,1)} copy(bf16[4,4,8,8,512]{4,3,2,1,0:T(8,128)(2,1)} %bitcast.8) | data formatting | bytes 2097152 | tf_op jit(solution)/shard_map/reshape | solution.py:97
  174.5 2.9 %gather_fusion.1 = bf16[32,32,512]{2,1,0:T(8,128)(2,1)} fusion(bf16[4,32,8,512]{3,1,2,0:T(8,128)(2,1)} %bitcast.35, s32[32]{0:T(128)S(1)} %fusion.37), kind=kCustom, calls=%fused_computation.1 | custom fusion | bytes 2097408 | tf_op jit(solution)/shard_map/gather | solution.py:98
  177.4 12.3 %all-to-all-done.2 = bf16[32,32,512]{2,1,0:T(8,128)(2,1)S(1)} async-done(((bf16[32,32,512]{2,1,0:T(8,128)(2,1)}), bf16[32,32,512]{2,1,0:T(8,128)(2,1)S(1)}, u32[]{:S(2)}, u32[]{:S(2)}) %all-to-all-start.2) | async-done | bytes 1048608 | tf_op jit(solution)/shard_map/all_to_all | solution.py:99
  189.7 5.6 %all-to-all-start.5 = ((bf16[32,32,512]{2,1,0:T(8,128)(2,1)}), bf16[32,32,512]{2,1,0:T(8,128)(2,1)}, u32[]{:S(2)}, u32[]{:S(2)}) async-start(bf16[32,32,512]{2,1,0:T(8,128)(2,1)} %gather_fusion.1), calls=%async_computation.5 | async-start | bytes 2097152 | tf_op jit(solution)/shard_map/all_to_all | solution.py:99
  195.4 17.3 %all-to-all-done.5 = bf16[32,32,512]{2,1,0:T(8,128)(2,1)} async-done(((bf16[32,32,512]{2,1,0:T(8,128)(2,1)}), bf16[32,32,512]{2,1,0:T(8,128)(2,1)}, u32[]{:S(2)}, u32[]{:S(2)}) %all-to-all-start.5) | async-done | bytes 1048608 | tf_op jit(solution)/shard_map/all_to_all | solution.py:99
  212.7 1.4 convert_reduce_fusion
  214.1 0.7 maximum_multiply_fusion
  (19 shorter events, 0.4 us)
Async XLA Ops:
  0.0 119.4 %copy-start = (bf16[4096,256]{1,0:T(8,128)(2,1)S(1)}, bf16[4096,256]{1,0:T(8,128)(2,1)}, u32[]{:S(2)}) copy-start(bf16[4096,256]{1,0:T(8,128)(2,1)} %param.8) | copy-start | bytes 6291460
  13.1 19.0 %copy-start.2 = (s32[8192]{0:T(1024)S(1)}, s32[8192]{0:T(1024)}, u32[]{:S(2)}) copy-start(s32[8192]{0:T(1024)} %param.7) | copy-start | bytes 98308
  53.1 49.5 %all-to-all-start = ((bf16[32,32,256]{2,1,0:T(8,128)(2,1)}), bf16[32,32,256]{2,1,0:T(8,128)(2,1)S(1)}, u32[]{:S(2)}, u32[]{:S(2)}) async-start(bf16[32,32,256]{2,1,0:T(8,128)(2,1)} %copy.37), calls=%async_computation | async-start | bytes 1048576 | tf_op jit(solution)/shard_map/all_to_all | solution.py:80
  79.8 70.5 %copy-start.3 = (s32[32]{0:T(128)S(1)}, s32[32]{0:T(128)}, u32[]{:S(2)}) copy-start(s32[32]{0:T(128)} %param.9) | copy-start | bytes 388
  102.6 21.7 %all-to-all-start.3 = ((bf16[32,32,256]{2,1,0:T(8,128)(2,1)}), bf16[32,32,256]{2,1,0:T(8,128)(2,1)S(1)}, u32[]{:S(2)}, u32[]{:S(2)}) async-start(bf16[32,32,256]{2,1,0:T(8,128)(2,1)} %copy.42), calls=%async_computation.3 | async-start | bytes 1048576 | tf_op jit(solution)/shard_map/all_to_all | solution.py:80
  124.3 0.8 copy-start.1
  125.1 20.9 %all-to-all-start.1 = ((bf16[4,32,4096]{2,1,0:T(8,128)(2,1)}), bf16[4,32,4096]{2,1,0:T(8,128)(2,1)S(1)}, u32[]{:S(2)}, u32[]{:S(2)}) async-start(bf16[4,32,4096]{2,1,0:T(8,128)(2,1)} %bitcast.3), calls=%async_computation.1 | async-start | bytes 2097152 | tf_op jit(solution)/shard_map/all_to_all | solution.py:87
  146.0 18.8 %all-to-all-start.4 = ((bf16[4,32,4096]{2,1,0:T(8,128)(2,1)}), bf16[4,32,4096]{2,1,0:T(8,128)(2,1)}, u32[]{:S(2)}, u32[]{:S(2)}) async-start(bf16[4,32,4096]{2,1,0:T(8,128)(2,1)} %bitcast.5), calls=%async_computation.4 | async-start | bytes 2097152 | tf_op jit(solution)/shard_map/all_to_all | solution.py:87
  164.8 24.9 %all-to-all-start.2 = ((bf16[32,32,512]{2,1,0:T(8,128)(2,1)}), bf16[32,32,512]{2,1,0:T(8,128)(2,1)S(1)}, u32[]{:S(2)}, u32[]{:S(2)}) async-start(bf16[32,32,512]{2,1,0:T(8,128)(2,1)} %gather_fusion), calls=%async_computation.2 | async-start | bytes 2097152 | tf_op jit(solution)/shard_map/all_to_all | solution.py:99
  189.7 23.0 %all-to-all-start.5 = ((bf16[32,32,512]{2,1,0:T(8,128)(2,1)}), bf16[32,32,512]{2,1,0:T(8,128)(2,1)}, u32[]{:S(2)}, u32[]{:S(2)}) async-start(bf16[32,32,512]{2,1,0:T(8,128)(2,1)} %gather_fusion.1), calls=%async_computation.5 | async-start | bytes 2097152 | tf_op jit(solution)/shard_map/all_to_all | solution.py:99

commit v5 on v3

--- a/solution.py
+++ b/solution.py
@@ -75,21 +75,18 @@
     projected = (jnp.sum(returned.astype(jnp.float32), axis=0) * cross).astype(jnp.bfloat16)
 
     every = lax.all_gather(projected, "ex", axis=0, tiled=True)
-    partial_value = lax.dot_general(
-        every, queries, (((1,), (1,)), ((), ())), preferred_element_type=jnp.float32
-    )
     ex_count = lax.axis_size("ex")
-    mine = lax.all_to_all(
-        partial_value.astype(jnp.bfloat16).reshape(ex_count, examples, -1),
-        "ex",
-        split_axis=0,
-        concat_axis=0,
-        tiled=True,
-    )
     panel_count = panel_order.shape[0]
     per_row = panel_count // ex_count
-    mine = mine.reshape(ex_count, examples, per_row, -1)
-    ordered = mine[panel_order // per_row, :, panel_order % per_row, :]
+    partial_value = lax.dot_general(
+        every.reshape(ex_count, examples, -1),
+        queries.reshape(per_row, -1, queries.shape[1]),
+        (((2,), (2,)), ((), ())),
+        preferred_element_type=jnp.float32,
+    )
+    partial_value = jnp.transpose(partial_value, (0, 2, 1, 3)).astype(jnp.bfloat16)
+    mine = lax.all_to_all(partial_value, "ex", split_axis=0, concat_axis=0, tiled=True)
+    ordered = mine[panel_order // per_row, panel_order % per_row]
     gathered = lax.all_to_all(ordered, "feat", split_axis=0, concat_axis=0, tiled=True)
     summed_scores = jnp.sum(gathered.astype(jnp.float32), axis=0)
     return summed_scores * (1.0 / math.sqrt(PROJ))

time: 165 us -> 162 us (0.982)
  local copies, waits for them, and re-layouts: 18.5 us -> 15.3 us
    reshape x1 -> x0, local copies, waits for them, and re-layouts: 3.19 us -> none  [on_device(): mine = mine.reshape(ex_count, examples, per_row, -1)]
where the time goes in v5:
time: 162 us; the launch traced here: 161 us
  blocking collectives  68.5 us (42%)
  matrix products  36.6 us (23%)
  waiting for transfers between devices  25.7 us (16%)
  local copies, waits for them, and re-layouts  15.3 us (9%)
  other arithmetic  10.9 us (7%)
  starting transfers between devices  4.43 us (3%)
    all_to_all x1, blocking collectives, on_device(): lax.all_to_all(ordered, 'feat', split_axis=0, concat_axis=0, tiled=True)  34.4 us
    all_to_all x1, blocking collectives, on_device(): lax.all_to_all(outgoing, 'feat', split_axis=0, concat_axis=0, tiled=True)  28.7 us
    all_to_all x1, waiting for transfers between devices, on_device(): lax.all_to_all(partial_value, 'ex', split_axis=0, concat_axis=0, tiled=True)  25.7 us
    dot_general x1, matrix products, on_device(): lax.dot_general(turned.astype(jnp.bfloat16), rows, (((2,), (2,)), ((0,),...  20.6 us
    dot_general x1, matrix products, on_device(): jnp.einsum('ca,eab->ceb', table_a, signed.reshape(examples, HA, HB), pref...  14 us
    unnamed x7, local copies, waits for them, and re-layouts  8.79 us
    mul x1, other arithmetic, on_device(): signed = grads * (1 - 2 * sign_bits).astype(jnp.bfloat16)[None, :]  8.52 us
    all_gather x1, blocking collectives, on_device(): every = lax.all_gather(projected, 'ex', axis=0, tiled=True)  5.42 us
  transfers between devices with their start and end apart: 1, of which 1 were waited for; matrix products, arithmetic and copies ran while one was open for 0% of the time, Pallas kernels for 0%

profile of v5, /device:TPU:8, one launch (start us, length us, event | category | flops | bytes accessed | tf_op | source)
XLA Modules:
  0.0 161.5 jit_solution(17834026389811392558)
XLA Ops:
  0.0 0.0 copy-start
  0.0 1.2 subtract_convert_fusion
  1.3 8.5 %broadcast_multiply_fusion = bf16[64,131072]{1,0:T(8,128)(2,1)S(1)} fusion(bf16[64,131072]{1,0:T(8,128)(2,1)} %param.5, bf16[131072]{0:T(1024)(128)(2,1)S(1)} %subtract_convert_fusion), kind=kLoop, calls=%fused_computation.22 | loop fusion | flops 8388608 | bytes 33816576 | tf_op jit(solution)/shard_map/mul | solution.py:55
  9.8 8.8 %copy.24 = bf16[8,8,256,512]{3,2,1,0:T(8,128)(2,1)} copy(bf16[8,8,256,512]{3,1,2,0:T(8,128)(2,1)S(1)} %bitcast.24) | data formatting | bytes 33554432
  18.6 0.0 copy-start.1
  18.6 14.0 %convolution_convert_fusion = bf16[256,64,512]{2,0,1:T(8,128)(2,1)} fusion(bf16[64,256,512]{2,1,0:T(8,128)(2,1)} %bitcast.23), kind=kOutput, calls=%fused_computation.14 | convolution fusion | flops 4305256448 | bytes 33554432 | tf_op jit(solution)/shard_map/ca,eab->ceb/dot_general | solution.py:57
  32.5 0.0 copy-done.1
  32.6 0.1 copy.17
  32.7 0.0 copy-start.2
  32.7 20.6 %multiply_bitcast_fusion = bf16[32,64,256]{1,0,2:T(8,128)(2,1)} fusion(s32[32,256]{0,1:T(8,128)S(1)} %copy.17, bf16[256,64,512]{2,0,1:T(8,128)(2,1)} %convolution_convert_fusion, bf16[32]{0:T(256)(128)(2,1)S(1)} %convert_bitcast_fusion.1), kind=kOutput, calls=%fused_computation.26 | convolution fusion | flops 609222656 | bytes 17858624 | tf_op jit(solution)/shard_map/dot_general | solution.py:64
  53.3 2.8 %copy.19 = bf16[32,64,256]{2,1,0:T(8,128)(2,1)S(1)} copy(bf16[32,64,256]{1,0,2:T(8,128)(2,1)} %multiply_bitcast_fusion) | data formatting | bytes 2097152 | tf_op jit(solution)/shard_map/mul | solution.py:73
  56.1 28.7 %all_to_all.15 = bf16[32,64,256]{2,1,0:T(8,128)(2,1)S(1)} all-to-all(bf16[32,64,256]{2,1,0:T(8,128)(2,1)S(1)} %copy.19), channel_id=1, replica_groups=mesh['feat'=32,'ex'=4] {'feat'}, dimensions={0} | all-to-all | bytes 2097152 | tf_op jit(solution)/shard_map/all_to_all | solution.py:74
  84.8 0.2 convert_reduce_fusion.1
  84.9 5.4 %all_gather.3 = bf16[256,256]{1,0:T(8,128)(2,1)S(1)} all-gather(bf16[64,256]{1,0:T(8,128)(2,1)S(1)} %multiply_convert_fusion.1), channel_id=1, replica_groups=mesh['feat'=32,'ex'=4] {'ex'}, dimensions={0}, use_global_device_ids=true | all-gather | bytes 163840 | tf_op jit(solution)/shard_map/all_gather | solution.py:77
  90.4 0.0 copy-done
  90.4 2.1 %convert_bitcast_fusion = bf16[4,8,64,512]{3,2,1,0:T(8,128)(2,1)} fusion(bf16[4,64,256,1]{2,1,3,0:T(8,128)(2,1)S(1)} %bitcast.25, bf16[8,512,256,1]{2,1,0,3:T(8,128)(2,1)S(1)} %bitcast.22), kind=kOutput, calls=%fused_computation.24 | convolution fusion | flops 537919488 | bytes 4325376 | tf_op jit(solution)/shard_map/dot_general | solution.py:81
  92.4 4.4 %all-to-all-start.1 = ((bf16[4,8,64,512]{3,2,1,0:T(8,128)(2,1)}), bf16[4,8,64,512]{3,2,1,0:T(8,128)(2,1)}, u32[]{:S(2)}, u32[]{:S(2)}) async-start(bf16[4,8,64,512]{3,2,1,0:T(8,128)(2,1)} %convert_bitcast_fusion), calls=%async_computation.1 | async-start | bytes 4194304 | tf_op jit(solution)/shard_map/all_to_all | solution.py:88
  96.8 0.0 copy-done.2
  96.9 25.7 %all-to-all-done.1 = bf16[4,8,64,512]{3,2,1,0:T(8,128)(2,1)} async-done(((bf16[4,8,64,512]{3,2,1,0:T(8,128)(2,1)}), bf16[4,8,64,512]{3,2,1,0:T(8,128)(2,1)}, u32[]{:S(2)}, u32[]{:S(2)}) %all-to-all-start.1) | async-done | bytes 2097184 | tf_op jit(solution)/shard_map/all_to_all | solution.py:88
  122.6 3.6 %gather_fusion = bf16[32,64,512]{2,1,0:T(8,128)(2,1)} fusion(bf16[4,8,64,512]{3,2,1,0:T(8,128)(2,1)} %all-to-all-done.1, s32[32]{0:T(128)S(1)} %fusion.38), kind=kCustom, calls=%fused_computation | custom fusion | bytes 4194560 | tf_op jit(solution)/shard_map/gather | solution.py:89
  126.2 34.4 %all_to_all.16 = bf16[32,64,512]{2,1,0:T(8,128)(2,1)S(1)} all-to-all(bf16[32,64,512]{2,1,0:T(8,128)(2,1)} %gather_fusion), channel_id=1, replica_groups=mesh['feat'=32,'ex'=4] {'feat'}, dimensions={0} | all-to-all | bytes 4194304 | tf_op jit(solution)/shard_map/all_to_all | solution.py:90
  160.5 0.3 convert_reduce_fusion
  160.8 0.7 broadcast_multiply_fusion.1
  (6 shorter events, 0.1 us)
Async XLA Ops:
  0.0 90.4 %copy-start = (bf16[4096,256]{1,0:T(8,128)(2,1)S(1)}, bf16[4096,256]{1,0:T(8,128)(2,1)}, u32[]{:S(2)}) copy-start(bf16[4096,256]{1,0:T(8,128)(2,1)} %param.8) | copy-start | bytes 6291460
  18.6 14.0 %copy-start.1 = (s32[8192]{0:T(1024)S(1)}, s32[8192]{0:T(1024)}, u32[]{:S(2)}) copy-start(s32[8192]{0:T(1024)} %param.7) | copy-start | bytes 98308
  32.7 64.2 %copy-start.2 = (s32[32]{0:T(128)S(1)}, s32[32]{0:T(128)}, u32[]{:S(2)}) copy-start(s32[32]{0:T(128)} %param.9) | copy-start | bytes 388
  92.4 30.2 %all-to-all-start.1 = ((bf16[4,8,64,512]{3,2,1,0:T(8,128)(2,1)}), bf16[4,8,64,512]{3,2,1,0:T(8,128)(2,1)}, u32[]{:S(2)}, u32[]{:S(2)}) async-start(bf16[4,8,64,512]{3,2,1,0:T(8,128)(2,1)} %convert_bitcast_fusion), calls=%async_computation.1 | async-start | bytes 4194304 | tf_op jit(solution)/shard_map/all_to_all | solution.py:88

commit v6 on v5

--- a/solution.py
+++ b/solution.py
@@ -84,12 +84,12 @@
         (((2,), (2,)), ((), ())),
         preferred_element_type=jnp.float32,
     )
-    partial_value = jnp.transpose(partial_value, (0, 2, 1, 3)).astype(jnp.bfloat16)
+    partial_value = jnp.transpose(partial_value * (1.0 / math.sqrt(PROJ)), (0, 2, 1, 3))
+    partial_value = partial_value.astype(jnp.bfloat16)
     mine = lax.all_to_all(partial_value, "ex", split_axis=0, concat_axis=0, tiled=True)
-    ordered = mine[panel_order // per_row, panel_order % per_row]
+    ordered = jnp.take(mine.reshape(panel_count, examples, -1), panel_order, axis=0, mode="clip")
     gathered = lax.all_to_all(ordered, "feat", split_axis=0, concat_axis=0, tiled=True)
-    summed_scores = jnp.sum(gathered.astype(jnp.float32), axis=0)
-    return summed_scores * (1.0 / math.sqrt(PROJ))
+    return jnp.sum(gathered.astype(jnp.float32), axis=0)
 
 
 def solution(mesh):

time: 162 us -> 162 us (level)
  no operation moved by 1% of the time
where the time goes in v6:
time: 162 us; the launch traced here: 161 us
  blocking collectives  68.5 us (42%)
  matrix products  36.6 us (23%)
  waiting for transfers between devices  25.7 us (16%)
  local copies, waits for them, and re-layouts  15.3 us (9%)
  other arithmetic  10.9 us (7%)
  starting transfers between devices  4.43 us (3%)
    all_to_all x1, blocking collectives, on_device(): lax.all_to_all(ordered, 'feat', split_axis=0, concat_axis=0, tiled=True)  34.4 us
    all_to_all x1, blocking collectives, on_device(): lax.all_to_all(outgoing, 'feat', split_axis=0, concat_axis=0, tiled=True)  28.7 us
    all_to_all x1, waiting for transfers between devices, on_device(): lax.all_to_all(partial_value, 'ex', split_axis=0, concat_axis=0, tiled=True)  25.7 us
    dot_general x1, matrix products, on_device(): lax.dot_general(turned.astype(jnp.bfloat16), rows, (((2,), (2,)), ((0,),...  20.6 us
    dot_general x1, matrix products, on_device(): jnp.einsum('ca,eab->ceb', table_a, signed.reshape(examples, HA, HB), pref...  14 us
    unnamed x7, local copies, waits for them, and re-layouts  8.79 us
    mul x1, other arithmetic, on_device(): signed = grads * (1 - 2 * sign_bits).astype(jnp.bfloat16)[None, :]  8.52 us
    all_gather x1, blocking collectives, on_device(): every = lax.all_gather(projected, 'ex', axis=0, tiled=True)  5.42 us
  transfers between devices with their start and end apart: 1, of which 1 were waited for; matrix products, arithmetic and copies ran while one was open for 0% of the time, Pallas kernels for 0%

profile of v6, /device:TPU:8, one launch (start us, length us, event | category | flops | bytes accessed | tf_op | source)
XLA Modules:
  0.0 161.5 jit_solution(10771877939283327149)
XLA Ops:
  0.0 0.0 copy-start
  0.0 1.2 subtract_convert_fusion
  1.3 8.5 %broadcast_multiply_fusion = bf16[64,131072]{1,0:T(8,128)(2,1)S(1)} fusion(bf16[64,131072]{1,0:T(8,128)(2,1)} %param.5, bf16[131072]{0:T(1024)(128)(2,1)S(1)} %subtract_convert_fusion), kind=kLoop, calls=%fused_computation.22 | loop fusion | flops 8388608 | bytes 33816576 | tf_op jit(solution)/shard_map/mul | solution.py:55
  9.8 8.8 %copy.24 = bf16[8,8,256,512]{3,2,1,0:T(8,128)(2,1)} copy(bf16[8,8,256,512]{3,1,2,0:T(8,128)(2,1)S(1)} %bitcast.25) | data formatting | bytes 33554432
  18.6 0.0 copy-start.1
  18.6 14.0 %convolution_convert_fusion = bf16[256,64,512]{2,0,1:T(8,128)(2,1)} fusion(bf16[64,256,512]{2,1,0:T(8,128)(2,1)} %bitcast.24), kind=kOutput, calls=%fused_computation.14 | convolution fusion | flops 4305256448 | bytes 33554432 | tf_op jit(solution)/shard_map/ca,eab->ceb/dot_general | solution.py:57
  32.5 0.0 copy-done.1
  32.6 0.1 copy.17
  32.7 0.0 copy-start.2
  32.7 20.6 %multiply_bitcast_fusion = bf16[32,64,256]{1,0,2:T(8,128)(2,1)} fusion(s32[32,256]{0,1:T(8,128)S(1)} %copy.17, bf16[256,64,512]{2,0,1:T(8,128)(2,1)} %convolution_convert_fusion, bf16[32]{0:T(256)(128)(2,1)S(1)} %convert_bitcast_fusion), kind=kOutput, calls=%fused_computation.26 | convolution fusion | flops 609222656 | bytes 17858624 | tf_op jit(solution)/shard_map/dot_general | solution.py:64
  53.3 2.8 %copy.19 = bf16[32,64,256]{2,1,0:T(8,128)(2,1)S(1)} copy(bf16[32,64,256]{1,0,2:T(8,128)(2,1)} %multiply_bitcast_fusion) | data formatting | bytes 2097152 | tf_op jit(solution)/shard_map/mul | solution.py:73
  56.1 28.7 %all_to_all.15 = bf16[32,64,256]{2,1,0:T(8,128)(2,1)S(1)} all-to-all(bf16[32,64,256]{2,1,0:T(8,128)(2,1)S(1)} %copy.19), channel_id=1, replica_groups=mesh['feat'=32,'ex'=4] {'feat'}, dimensions={0} | all-to-all | bytes 2097152 | tf_op jit(solution)/shard_map/all_to_all | solution.py:74
  84.8 0.2 convert_reduce_fusion.1
  84.9 5.4 %all_gather.3 = bf16[256,256]{1,0:T(8,128)(2,1)S(1)} all-gather(bf16[64,256]{1,0:T(8,128)(2,1)S(1)} %multiply_convert_fusion.2), channel_id=1, replica_groups=mesh['feat'=32,'ex'=4] {'ex'}, dimensions={0}, use_global_device_ids=true | all-gather | bytes 163840 | tf_op jit(solution)/shard_map/all_gather | solution.py:77
  90.4 0.0 copy-done
  90.4 2.1 %fusion.20 = bf16[4,8,64,512]{3,2,1,0:T(8,128)(2,1)} fusion(bf16[4,64,256,1]{2,1,3,0:T(8,128)(2,1)S(1)} %bitcast.26, bf16[8,512,256,1]{2,1,0,3:T(8,128)(2,1)S(1)} %bitcast.23), kind=kOutput, calls=%fused_computation.27 | convolution fusion | flops 538968064 | bytes 4325376 | tf_op jit(solution)/shard_map/dot_general | solution.py:81
  92.4 4.4 %all-to-all-start.1 = ((bf16[4,8,64,512]{3,2,1,0:T(8,128)(2,1)}), bf16[4,8,64,512]{3,2,1,0:T(8,128)(2,1)}, u32[]{:S(2)}, u32[]{:S(2)}) async-start(bf16[4,8,64,512]{3,2,1,0:T(8,128)(2,1)} %fusion.20), calls=%async_computation.1 | async-start | bytes 4194304 | tf_op jit(solution)/shard_map/all_to_all | solution.py:89
  96.8 0.0 copy-done.2
  96.9 25.7 %all-to-all-done.1 = bf16[4,8,64,512]{3,2,1,0:T(8,128)(2,1)} async-done(((bf16[4,8,64,512]{3,2,1,0:T(8,128)(2,1)}), bf16[4,8,64,512]{3,2,1,0:T(8,128)(2,1)}, u32[]{:S(2)}, u32[]{:S(2)}) %all-to-all-start.1) | async-done | bytes 2097184 | tf_op jit(solution)/shard_map/all_to_all | solution.py:89
  122.6 3.6 %gather_fusion = bf16[32,64,512]{2,1,0:T(8,128)(2,1)} fusion(bf16[32,64,512]{2,1,0:T(8,128)(2,1)} %bitcast.9, s32[1024]{0:T(1024)S(1)} %pad_clamp_fusion), kind=kCustom, calls=%fused_computation | custom fusion | bytes 4194432 | tf_op jit(solution)/shard_map/jit(_take)/gather | solution.py:90
  126.2 34.4 %all_to_all.16 = bf16[32,64,512]{2,1,0:T(8,128)(2,1)S(1)} all-to-all(bf16[32,64,512]{2,1,0:T(8,128)(2,1)} %gather_fusion), channel_id=1, replica_groups=mesh['feat'=32,'ex'=4] {'feat'}, dimensions={0} | all-to-all | bytes 4194304 | tf_op jit(solution)/shard_map/all_to_all | solution.py:91
  160.5 0.9 convert_reduce_fusion
  (6 shorter events, 0.1 us)
Async XLA Ops:
  0.0 90.4 %copy-start = (bf16[4096,256]{1,0:T(8,128)(2,1)S(1)}, bf16[4096,256]{1,0:T(8,128)(2,1)}, u32[]{:S(2)}) copy-start(bf16[4096,256]{1,0:T(8,128)(2,1)} %param.8) | copy-start | bytes 6291460
  18.6 14.0 %copy-start.1 = (s32[8192]{0:T(1024)S(1)}, s32[8192]{0:T(1024)}, u32[]{:S(2)}) copy-start(s32[8192]{0:T(1024)} %param.7) | copy-start | bytes 98308
  32.7 64.2 %copy-start.2 = (s32[32]{0:T(128)S(1)}, s32[32]{0:T(128)}, u32[]{:S(2)}) copy-start(s32[32]{0:T(128)} %param.9) | copy-start | bytes 388
  92.4 30.2 %all-to-all-start.1 = ((bf16[4,8,64,512]{3,2,1,0:T(8,128)(2,1)}), bf16[4,8,64,512]{3,2,1,0:T(8,128)(2,1)}, u32[]{:S(2)}, u32[]{:S(2)}) async-start(bf16[4,8,64,512]{3,2,1,0:T(8,128)(2,1)} %fusion.20), calls=%async_computation.1 | async-start | bytes 4194304 | tf_op jit(solution)/shard_map/all_to_all | solution.py:89

commit v7 on v6

--- a/solution.py
+++ b/solution.py
@@ -52,14 +52,11 @@
     cross = power_scale(feat_dev * shards) / (scale_a * scale_b)
     device_id = lax.axis_index("feat")
 
-    signed = grads * (1 - 2 * sign_bits).astype(jnp.bfloat16)[None, :]
+    flips = (1 - 2 * sign_bits).astype(jnp.bfloat16).reshape(1, 1, HA, HB)
+    signed = grads.reshape(examples // 8, 8, HA, HB) * flips
     table_a = hadamard_table(HA, scale_a, jnp.bfloat16)
-    turned = jnp.einsum(
-        "ca,eab->ceb",
-        table_a,
-        signed.reshape(examples, HA, HB),
-        preferred_element_type=jnp.float32,
-    )
+    turned = jnp.einsum("ca,tiab->ctib", table_a, signed, preferred_element_type=jnp.float32)
+    turned = turned.reshape(HA, examples, HB)
     rows = hadamard_rows(sample_offset.reshape(shards, proj_dev), HB, scale_b)
     picked = lax.dot_general(
         turned.astype(jnp.bfloat16),

time: 162 us -> 162 us (level)
  other arithmetic: 10.9 us -> 20 us
  local copies, waits for them, and re-layouts: 15.3 us -> 6.65 us
    mul x1, other arithmetic: 8.52 us -> 17.6 us  [on_device(): signed = grads.reshape(examples // 8, 8, HA, HB) * flips]
    unnamed x7 -> x6, local copies, waits for them, and re-layouts: 8.79 us -> 0.01 us
where the time goes in v7:
time: 162 us
  blocking collectives  68.5 us (42%)
  matrix products  36.6 us (23%)
  waiting for transfers between devices  25.7 us (16%)
  other arithmetic  20 us (12%)
  local copies, waits for them, and re-layouts  6.65 us (4%)
  starting transfers between devices  4.43 us (3%)
    all_to_all x1, blocking collectives, on_device(): lax.all_to_all(ordered, 'feat', split_axis=0, concat_axis=0, tiled=True)  34.4 us
    all_to_all x1, blocking collectives, on_device(): lax.all_to_all(outgoing, 'feat', split_axis=0, concat_axis=0, tiled=True)  28.7 us
    all_to_all x1, waiting for transfers between devices, on_device(): lax.all_to_all(partial_value, 'ex', split_axis=0, concat_axis=0, tiled=True)  25.7 us
    dot_general x1, matrix products, on_device(): lax.dot_general(turned.astype(jnp.bfloat16), rows, (((2,), (2,)), ((0,),...  20.6 us
    mul x1, other arithmetic, on_device(): signed = grads.reshape(examples // 8, 8, HA, HB) * flips  17.6 us
    dot_general x1, matrix products, on_device(): jnp.einsum('ca,tiab->ctib', table_a, signed, preferred_element_type=jnp.f...  14 us
    all_gather x1, blocking collectives, on_device(): every = lax.all_gather(projected, 'ex', axis=0, tiled=True)  5.42 us
    all_to_all x1, starting transfers between devices, on_device(): lax.all_to_all(partial_value, 'ex', split_axis=0, concat_axis=0, tiled=True)  4.43 us
  transfers between devices with their start and end apart: 1, of which 1 were waited for; matrix products, arithmetic and copies ran while one was open for 0% of the time, Pallas kernels for 0%

profile of v7, /device:TPU:8, one launch (start us, length us, event | category | flops | bytes accessed | tf_op | source)
XLA Modules:
  0.0 162.0 jit_solution(6101999879627391211)
XLA Ops:
  0.0 0.0 copy-start
  0.0 1.2 subtract_convert_fusion
  1.3 0.2 mul.69
  1.5 17.6 %bitcast_multiply_fusion = bf16[8,8,256,512]{3,2,1,0:T(8,128)(2,1)} fusion(bf16[8,8,256,512]{3,1,2,0:T(8,128)(2,1)} %bitcast.31, bf16[256,512]{1,0:T(8,128)(2,1)S(1)} %mul.69), kind=kLoop, calls=%fused_computation.11 | loop fusion | flops 8388608 | bytes 33816576 | tf_op jit(solution)/shard_map/mul | solution.py:56
  19.1 0.0 copy-start.1
  19.1 14.0 %convolution_convert_fusion = bf16[256,64,512]{2,0,1:T(8,128)(2,1)} fusion(bf16[64,512,256]{1,2,0:T(8,128)(2,1)} %bitcast.30), kind=kOutput, calls=%fused_computation.15 | convolution fusion | flops 4305256448 | bytes 33554432 | tf_op jit(solution)/shard_map/ca,tiab->ctib/dot_general | solution.py:58
  33.0 0.0 copy-done.1
  33.0 0.1 copy.23
  33.2 0.0 copy-start.2
  33.2 20.6 %multiply_bitcast_fusion = bf16[32,64,256]{1,0,2:T(8,128)(2,1)} fusion(s32[32,256]{0,1:T(8,128)S(1)} %copy.23, bf16[256,64,512]{2,0,1:T(8,128)(2,1)} %convolution_convert_fusion, bf16[32]{0:T(256)(128)(2,1)S(1)} %convert_bitcast_fusion), kind=kOutput, calls=%fused_computation.26 | convolution fusion | flops 609222656 | bytes 17858624 | tf_op jit(solution)/shard_map/dot_general | solution.py:61
  53.8 2.8 %copy.25 = bf16[32,64,256]{2,1,0:T(8,128)(2,1)S(1)} copy(bf16[32,64,256]{1,0,2:T(8,128)(2,1)} %multiply_bitcast_fusion) | data formatting | bytes 2097152 | tf_op jit(solution)/shard_map/mul | solution.py:70
  56.6 28.7 %all_to_all.15 = bf16[32,64,256]{2,1,0:T(8,128)(2,1)S(1)} all-to-all(bf16[32,64,256]{2,1,0:T(8,128)(2,1)S(1)} %copy.25), channel_id=1, replica_groups=mesh['feat'=32,'ex'=4] {'feat'}, dimensions={0} | all-to-all | bytes 2097152 | tf_op jit(solution)/shard_map/all_to_all | solution.py:71
  85.2 0.2 convert_reduce_fusion.1
  85.4 5.4 %all_gather.3 = bf16[256,256]{1,0:T(8,128)(2,1)S(1)} all-gather(bf16[64,256]{1,0:T(8,128)(2,1)S(1)} %multiply_convert_fusion.2), channel_id=1, replica_groups=mesh['feat'=32,'ex'=4] {'ex'}, dimensions={0}, use_global_device_ids=true | all-gather | bytes 163840 | tf_op jit(solution)/shard_map/all_gather | solution.py:74
  90.8 0.0 copy-done
  90.8 2.1 %fusion.20 = bf16[4,8,64,512]{3,2,1,0:T(8,128)(2,1)} fusion(bf16[4,64,256,1]{2,1,3,0:T(8,128)(2,1)S(1)} %bitcast.32, bf16[8,512,256,1]{2,1,0,3:T(8,128)(2,1)S(1)} %bitcast.29), kind=kOutput, calls=%fused_computation.27 | convolution fusion | flops 538968064 | bytes 4325376 | tf_op jit(solution)/shard_map/dot_general | solution.py:78
  92.9 4.4 %all-to-all-start.1 = ((bf16[4,8,64,512]{3,2,1,0:T(8,128)(2,1)}), bf16[4,8,64,512]{3,2,1,0:T(8,128)(2,1)}, u32[]{:S(2)}, u32[]{:S(2)}) async-start(bf16[4,8,64,512]{3,2,1,0:T(8,128)(2,1)} %fusion.20), calls=%async_computation.1 | async-start | bytes 4194304 | tf_op jit(solution)/shard_map/all_to_all | solution.py:86
  97.3 0.0 copy-done.2
  97.4 25.7 %all-to-all-done.1 = bf16[4,8,64,512]{3,2,1,0:T(8,128)(2,1)} async-done(((bf16[4,8,64,512]{3,2,1,0:T(8,128)(2,1)}), bf16[4,8,64,512]{3,2,1,0:T(8,128)(2,1)}, u32[]{:S(2)}, u32[]{:S(2)}) %all-to-all-start.1) | async-done | bytes 2097184 | tf_op jit(solution)/shard_map/all_to_all | solution.py:86
  123.1 3.6 %gather_fusion = bf16[32,64,512]{2,1,0:T(8,128)(2,1)} fusion(bf16[32,64,512]{2,1,0:T(8,128)(2,1)} %bitcast.11, s32[1024]{0:T(1024)S(1)} %pad_clamp_fusion), kind=kCustom, calls=%fused_computation | custom fusion | bytes 4194432 | tf_op jit(solution)/shard_map/jit(_take)/gather | solution.py:87
  126.6 34.4 %all_to_all.16 = bf16[32,64,512]{2,1,0:T(8,128)(2,1)S(1)} all-to-all(bf16[32,64,512]{2,1,0:T(8,128)(2,1)} %gather_fusion), channel_id=1, replica_groups=mesh['feat'=32,'ex'=4] {'feat'}, dimensions={0} | all-to-all | bytes 4194304 | tf_op jit(solution)/shard_map/all_to_all | solution.py:88
  161.0 0.9 convert_reduce_fusion
  (6 shorter events, 0.1 us)
Async XLA Ops:
  0.0 90.8 %copy-start = (bf16[4096,256]{1,0:T(8,128)(2,1)S(1)}, bf16[4096,256]{1,0:T(8,128)(2,1)}, u32[]{:S(2)}) copy-start(bf16[4096,256]{1,0:T(8,128)(2,1)} %param.8) | copy-start | bytes 6291460
  19.1 14.0 %copy-start.1 = (s32[8192]{0:T(1024)S(1)}, s32[8192]{0:T(1024)}, u32[]{:S(2)}) copy-start(s32[8192]{0:T(1024)} %param.7) | copy-start | bytes 98308
  33.2 64.2 %copy-start.2 = (s32[32]{0:T(128)S(1)}, s32[32]{0:T(128)}, u32[]{:S(2)}) copy-start(s32[32]{0:T(128)} %param.9) | copy-start | bytes 388
  92.9 30.2 %all-to-all-start.1 = ((bf16[4,8,64,512]{3,2,1,0:T(8,128)(2,1)}), bf16[4,8,64,512]{3,2,1,0:T(8,128)(2,1)}, u32[]{:S(2)}, u32[]{:S(2)}) async-start(bf16[4,8,64,512]{3,2,1,0:T(8,128)(2,1)} %fusion.20), calls=%async_computation.1 | async-start | bytes 4194304 | tf_op jit(solution)/shard_map/all_to_all | solution.py:86

commit v8 on v6

--- a/solution.py
+++ b/solution.py
@@ -60,13 +60,16 @@
         signed.reshape(examples, HA, HB),
         preferred_element_type=jnp.float32,
     )
-    rows = hadamard_rows(sample_offset.reshape(shards, proj_dev), HB, scale_b)
-    picked = lax.dot_general(
-        turned.astype(jnp.bfloat16),
-        rows,
-        (((2,), (2,)), ((0,), (1,))),
-        preferred_element_type=jnp.float32,
-    )
+    offsets = sample_offset.reshape(shards, proj_dev)
+    rows = hadamard_rows(offsets & (HB // 2 - 1), HB // 2, scale_b)
+    low, high = turned[..., : HB // 2], turned[..., HB // 2 :]
+    folded = jnp.stack([low + high, low - high], axis=1).astype(jnp.bfloat16)
+    folded = folded.reshape(HA, 2 * examples, HB // 2)
+    both = lax.dot_general(
+        folded, rows, (((2,), (2,)), ((0,), (1,))), preferred_element_type=jnp.float32
+    ).reshape(HA, 2, examples, shards)
+    top = jnp.transpose((offsets >> (HB.bit_length() - 2)) & 1)[:, None, :]
+    picked = jnp.where(top == 1, both[:, 1], both[:, 0])
     local = picked.astype(jnp.bfloat16)
     full_table = hadamard_table(shards, 1.0, jnp.bfloat16)
     signs = lax.dynamic_slice_in_dim(full_table, device_id, 1, 1)[:, 0]

time: 162 us -> 199 us (1.23)
  other arithmetic: 10.9 us -> 39.6 us
  matrix products: 36.6 us -> 42.4 us
  local copies, waits for them, and re-layouts: 15.3 us -> 17.9 us
    another operation x0 -> x2, other arithmetic: none -> 25.4 us  [on_device(): folded = jnp.stack([low + high, low - high], axis=1).astype(jnp.bfloat16)]
    dot_general x1, matrix products: 14 us -> 19 us  [on_device(): jnp.einsum('ca,eab->ceb', table_a, signed.reshape(examples, HA, HB), pref...]
    dot_general x0 -> x1, local copies, waits for them, and re-layouts: none -> 4.89 us  [on_device(): lax.dot_general(folded, rows, (((2,), (2,)), ((0,), (1,))), preferred_ele...]
    mul x1, local copies, waits for them, and re-layouts: 2.79 us -> 0.59 us  [on_device(): outgoing = jnp.transpose(local, (2, 1, 0)) * signs[:, None, None]]
    unnamed x7 -> x5, local copies, waits for them, and re-layouts: 8.79 us -> 8.7 us
where the time goes in v8:
time: 199 us
  blocking collectives  68.5 us (34%)
  matrix products  42.4 us (21%)
  other arithmetic  39.6 us (20%)
  waiting for transfers between devices  25.7 us (13%)
  local copies, waits for them, and re-layouts  17.9 us (9%)
  starting transfers between devices  4.43 us (2%)
    all_to_all x1, blocking collectives, on_device(): lax.all_to_all(ordered, 'feat', split_axis=0, concat_axis=0, tiled=True)  34.4 us
    all_to_all x1, blocking collectives, on_device(): lax.all_to_all(outgoing, 'feat', split_axis=0, concat_axis=0, tiled=True)  28.7 us
    all_to_all x1, waiting for transfers between devices, on_device(): lax.all_to_all(partial_value, 'ex', split_axis=0, concat_axis=0, tiled=True)  25.7 us
    another operation x2, other arithmetic, on_device(): folded = jnp.stack([low + high, low - high], axis=1).astype(jnp.bfloat16)  25.4 us
    dot_general x1, matrix products, on_device(): lax.dot_general(folded, rows, (((2,), (2,)), ((0,), (1,))), preferred_ele...  21.3 us
    dot_general x1, matrix products, on_device(): jnp.einsum('ca,eab->ceb', table_a, signed.reshape(examples, HA, HB), pref...  19 us
    unnamed x5, local copies, waits for them, and re-layouts  8.7 us
    mul x1, other arithmetic, on_device(): signed = grads * (1 - 2 * sign_bits).astype(jnp.bfloat16)[None, :]  8.52 us
  transfers between devices with their start and end apart: 1, of which 1 were waited for; matrix products, arithmetic and copies ran while one was open for 0% of the time, Pallas kernels for 0%

profile of v8, /device:TPU:8, one launch (start us, length us, event | category | flops | bytes accessed | tf_op | source)
XLA Modules:
  0.0 198.5 jit_solution(930930317716151417)
XLA Ops:
  0.0 0.0 copy-start
  0.0 0.9 broadcast_and_fusion
  0.9 0.8 and_compare_fusion
  1.7 1.1 subtract_convert_fusion.1
  2.8 8.5 %broadcast_multiply_fusion = bf16[64,131072]{1,0:T(8,128)(2,1)S(1)} fusion(bf16[64,131072]{1,0:T(8,128)(2,1)} %param.5, bf16[131072]{0:T(1024)(128)(2,1)S(1)} %subtract_convert_fusion.1), kind=kLoop, calls=%fused_computation.18 | loop fusion | flops 8388608 | bytes 33816576 | tf_op jit(solution)/shard_map/mul | solution.py:55
  11.4 8.7 %copy.16 = bf16[8,8,256,512]{3,2,1,0:T(8,128)(2,1)} copy(bf16[8,8,256,512]{3,1,2,0:T(8,128)(2,1)S(1)} %bitcast.50) | data formatting | bytes 33554432
  20.0 19.0 %fusion.23 = f32[256,64,512]{2,0,1:T(8,128)} fusion(bf16[64,256,512]{2,1,0:T(8,128)(2,1)} %bitcast.49), kind=kOutput, calls=%fused_computation.38 | convolution fusion | flops 4296867840 | bytes 50331648 | tf_op jit(solution)/shard_map/ca,eab->ceb/dot_general | solution.py:57
  39.0 17.4 %fusion.8 = (bf16[256,1,64,256]{3,0,2,1:T(8,128)(2,1)}, bf16[256,1,64,256]{3,0,2,1:T(8,128)(2,1)}) fusion(f32[256,64,512]{2,0,1:T(8,128)} %fusion.23), kind=kLoop, calls=%fused_computation.16 | loop fusion | flops 16777216 | bytes 50331648 | tf_op jit(solution)/shard_map/stack | solution.py:66
  56.4 0.1 copy.11
  56.5 8.0 %pad_maximum_fusion = bf16[256,2,64,256]{3,0,2,1:T(8,128)(2,1)S(1)} fusion(bf16[256,1,64,256]{3,0,2,1:T(8,128)(2,1)} %get-tuple-element.6, bf16[256,1,64,256]{3,0,2,1:T(8,128)(2,1)} %get-tuple-element.5), kind=kLoop, calls=%fused_computation.1 | loop fusion | flops 8388608 | bytes 33554432 | tf_op jit(solution)/shard_map/stack | solution.py:66
  64.5 21.3 %fusion = bf16[256,128,32]{1,2,0:T(8,128)(2,1)} fusion(bf16[256,128,256]{2,0,1:T(8,128)(2,1)S(1)} %bitcast.51, s32[32,256]{0,1:T(8,128)S(1)} %copy.11), kind=kOutput, calls=%fused_computation.2 | convolution fusion | flops 568328192 | bytes 18907136 | tf_op jit(solution)/shard_map/dot_general | solution.py:68
  85.9 4.9 %copy.13 = bf16[256,128,32]{0,2,1:T(8,128)(2,1)} copy(bf16[256,128,32]{1,2,0:T(8,128)(2,1)} %fusion) | data formatting | bytes 4194304 | tf_op jit(solution)/shard_map/dot_general | solution.py:68
  90.8 0.0 copy-start.1
  90.8 1.7 fusion.21
  92.5 0.6 copy.14
  93.1 28.7 %all_to_all.15 = bf16[32,64,256]{2,1,0:T(8,128)(2,1)S(1)} all-to-all(bf16[32,64,256]{2,1,0:T(8,128)(2,1)S(1)} %copy.14), channel_id=1, replica_groups=mesh['feat'=32,'ex'=4] {'feat'}, dimensions={0} | all-to-all | bytes 2097152 | tf_op jit(solution)/shard_map/all_to_all | solution.py:77
  121.8 0.2 convert_reduce_fusion.1
  121.9 5.4 %all_gather.3 = bf16[256,256]{1,0:T(8,128)(2,1)S(1)} all-gather(bf16[64,256]{1,0:T(8,128)(2,1)S(1)} %multiply_convert_fusion.2), channel_id=1, replica_groups=mesh['feat'=32,'ex'=4] {'ex'}, dimensions={0}, use_global_device_ids=true | all-gather | bytes 163840 | tf_op jit(solution)/shard_map/all_gather | solution.py:80
  127.4 0.0 copy-done
  127.4 2.1 %fusion.19 = bf16[4,8,64,512]{3,2,1,0:T(8,128)(2,1)} fusion(bf16[4,64,256,1]{2,1,3,0:T(8,128)(2,1)S(1)} %bitcast.53, bf16[8,512,256,1]{2,1,0,3:T(8,128)(2,1)S(1)} %bitcast.48), kind=kOutput, calls=%fused_computation.32 | convolution fusion | flops 538968064 | bytes 4325376 | tf_op jit(solution)/shard_map/dot_general | solution.py:84
  129.4 4.4 %all-to-all-start.1 = ((bf16[4,8,64,512]{3,2,1,0:T(8,128)(2,1)}), bf16[4,8,64,512]{3,2,1,0:T(8,128)(2,1)}, u32[]{:S(2)}, u32[]{:S(2)}) async-start(bf16[4,8,64,512]{3,2,1,0:T(8,128)(2,1)} %fusion.19), calls=%async_computation.1 | async-start | bytes 4194304 | tf_op jit(solution)/shard_map/all_to_all | solution.py:92
  133.9 0.0 copy-done.1
  133.9 25.7 %all-to-all-done.1 = bf16[4,8,64,512]{3,2,1,0:T(8,128)(2,1)} async-done(((bf16[4,8,64,512]{3,2,1,0:T(8,128)(2,1)}), bf16[4,8,64,512]{3,2,1,0:T(8,128)(2,1)}, u32[]{:S(2)}, u32[]{:S(2)}) %all-to-all-start.1) | async-done | bytes 2097184 | tf_op jit(solution)/shard_map/all_to_all | solution.py:92
  159.6 3.6 %gather_fusion = bf16[32,64,512]{2,1,0:T(8,128)(2,1)} fusion(bf16[32,64,512]{2,1,0:T(8,128)(2,1)} %bitcast.16, s32[1024]{0:T(1024)S(1)} %pad_clamp_fusion), kind=kCustom, calls=%fused_computation | custom fusion | bytes 4194432 | tf_op jit(solution)/shard_map/jit(_take)/gather | solution.py:93
  163.2 34.4 %all_to_all.16 = bf16[32,64,512]{2,1,0:T(8,128)(2,1)S(1)} all-to-all(bf16[32,64,512]{2,1,0:T(8,128)(2,1)} %gather_fusion), channel_id=1, replica_groups=mesh['feat'=32,'ex'=4] {'feat'}, dimensions={0} | all-to-all | bytes 4194304 | tf_op jit(solution)/shard_map/all_to_all | solution.py:94
  197.6 0.9 convert_reduce_fusion
  (7 shorter events, 0.1 us)
Async XLA Ops:
  0.0 127.4 %copy-start = (bf16[4096,256]{1,0:T(8,128)(2,1)S(1)}, bf16[4096,256]{1,0:T(8,128)(2,1)}, u32[]{:S(2)}) copy-start(bf16[4096,256]{1,0:T(8,128)(2,1)} %param.8) | copy-start | bytes 6291460
  90.8 43.1 %copy-start.1 = (s32[32]{0:T(128)S(1)}, s32[32]{0:T(128)}, u32[]{:S(2)}) copy-start(s32[32]{0:T(128)} %param.9) | copy-start | bytes 388
  129.4 30.2 %all-to-all-start.1 = ((bf16[4,8,64,512]{3,2,1,0:T(8,128)(2,1)}), bf16[4,8,64,512]{3,2,1,0:T(8,128)(2,1)}, u32[]{:S(2)}, u32[]{:S(2)}) async-start(bf16[4,8,64,512]{3,2,1,0:T(8,128)(2,1)} %fusion.19), calls=%async_computation.1 | async-start | bytes 4194304 | tf_op jit(solution)/shard_map/all_to_all | solution.py:92

commit v9 on v6

--- a/solution.py
+++ b/solution.py
@@ -74,8 +74,9 @@
     returned = lax.all_to_all(outgoing, "feat", split_axis=0, concat_axis=0, tiled=True)
     projected = (jnp.sum(returned.astype(jnp.float32), axis=0) * cross).astype(jnp.bfloat16)
 
-    every = lax.all_gather(projected, "ex", axis=0, tiled=True)
     ex_count = lax.axis_size("ex")
+    copies = jnp.broadcast_to(projected[None], (ex_count,) + projected.shape)
+    every = lax.all_to_all(copies, "ex", split_axis=0, concat_axis=0, tiled=True)
     panel_count = panel_order.shape[0]
     per_row = panel_count // ex_count
     partial_value = lax.dot_general(

time: 162 us -> 180 us (1.11)
  other arithmetic: 10.9 us -> 21.6 us
  matrix products: 36.6 us -> 42.1 us
    convert_element_type x0 -> x1, other arithmetic: none -> 10.6 us  [hadamard_rows(): return ((1 - 2 * parity).astype(jnp.float32) * scale).astype(jnp.bfloat16)]
    all_to_all x0 -> x1, blocking collectives: none -> 6.99 us  [on_device(): lax.all_to_all(copies, 'ex', split_axis=0, concat_axis=0, tiled=True)]
    dot_general x1, matrix products: 20.6 us -> 26.1 us  [on_device(): lax.dot_general(turned.astype(jnp.bfloat16), rows, (((2,), (2,)), ((0,),...]
    all_gather x1 -> x0, blocking collectives: 5.42 us -> none  [on_device(): every = lax.all_gather(projected, 'ex', axis=0, tiled=True)]
    dot_general x0 -> x1, local copies, waits for them, and re-layouts: none -> 2.8 us  [on_device(): lax.dot_general(turned.astype(jnp.bfloat16), rows, (((2,), (2,)), ((0,),...]
    mul x1 -> x0, local copies, waits for them, and re-layouts: 2.79 us -> none  [on_device(): outgoing = jnp.transpose(local, (2, 1, 0)) * signs[:, None, None]]
where the time goes in v9:
time: 180 us; the launch traced here: 179 us
  blocking collectives  70 us (39%)
  matrix products  42.1 us (23%)
  waiting for transfers between devices  25.7 us (14%)
  other arithmetic  21.6 us (12%)
  local copies, waits for them, and re-layouts  15.2 us (8%)
  starting transfers between devices  4.43 us (2%)
    all_to_all x1, blocking collectives, on_device(): lax.all_to_all(ordered, 'feat', split_axis=0, concat_axis=0, tiled=True)  34.4 us
    all_to_all x1, blocking collectives, on_device(): lax.all_to_all(outgoing, 'feat', split_axis=0, concat_axis=0, tiled=True)  28.7 us
    dot_general x1, matrix products, on_device(): lax.dot_general(turned.astype(jnp.bfloat16), rows, (((2,), (2,)), ((0,),...  26.1 us
    all_to_all x1, waiting for transfers between devices, on_device(): lax.all_to_all(partial_value, 'ex', split_axis=0, concat_axis=0, tiled=True)  25.7 us
    dot_general x1, matrix products, on_device(): jnp.einsum('ca,eab->ceb', table_a, signed.reshape(examples, HA, HB), pref...  13.9 us
    convert_element_type x1, other arithmetic, hadamard_rows(): return ((1 - 2 * parity).astype(jnp.float32) * scale).astype(jnp.bfloat16)  10.6 us
    unnamed x7, local copies, waits for them, and re-layouts  8.78 us
    mul x1, other arithmetic, on_device(): signed = grads * (1 - 2 * sign_bits).astype(jnp.bfloat16)[None, :]  8.52 us
  transfers between devices with their start and end apart: 1, of which 1 were waited for; matrix products, arithmetic and copies ran while one was open for 0% of the time, Pallas kernels for 0%

profile of v9, /device:TPU:8, one launch (start us, length us, event | category | flops | bytes accessed | tf_op | source)
XLA Modules:
  0.0 179.2 jit_solution(16965702583146081858)
XLA Ops:
  0.0 0.0 copy-start
  0.0 1.2 subtract_convert_fusion
  1.3 8.5 %broadcast_multiply_fusion = bf16[64,131072]{1,0:T(8,128)(2,1)S(1)} fusion(bf16[64,131072]{1,0:T(8,128)(2,1)} %param.5, bf16[131072]{0:T(1024)(128)(2,1)S(1)} %subtract_convert_fusion), kind=kLoop, calls=%fused_computation.15 | loop fusion | flops 8388608 | bytes 33816576 | tf_op jit(solution)/shard_map/mul | solution.py:55
  9.8 8.8 %copy.10 = bf16[8,8,256,512]{3,2,1,0:T(8,128)(2,1)} copy(bf16[8,8,256,512]{3,1,2,0:T(8,128)(2,1)S(1)} %bitcast.24) | data formatting | bytes 33554432
  18.6 0.0 copy-start.1
  18.6 13.9 %fusion.10 = bf16[256,64,512]{2,0,1:T(8,128)(2,1)} fusion(bf16[64,256,512]{2,1,0:T(8,128)(2,1)} %bitcast.23), kind=kOutput, calls=%fused_computation.24 | convolution fusion | flops 4296867840 | bytes 33554432 | tf_op jit(solution)/shard_map/ca,eab->ceb/dot_general | solution.py:57
  32.5 0.0 copy-done.1
  32.5 10.6 %fusion.6 = bf16[32,256,512]{2,1,0:T(8,128)(2,1)} fusion(s32[32,256]{1,0:T(8,128)S(1)} %and.95), kind=kLoop, calls=%fused_computation.13 | loop fusion | flops 71303168 | bytes 8421376 | tf_op jit(solution)/shard_map/convert_element_type | solution.py:29
  43.1 26.1 %fusion.5 = bf16[256,64,32]{1,2,0:T(8,128)(2,1)} fusion(bf16[256,64,512]{2,0,1:T(8,128)(2,1)} %fusion.10, bf16[32,256,512]{2,1,0:T(8,128)(2,1)} %fusion.6), kind=kOutput, calls=%fused_computation.12 | convolution fusion | flops 536870912 | bytes 26214400 | tf_op jit(solution)/shard_map/dot_general | solution.py:64
  69.3 0.0 copy-start.2
  69.3 2.8 %copy.8 = bf16[256,64,32]{0,1,2:T(8,128)(2,1)S(1)} copy(bf16[256,64,32]{1,2,0:T(8,128)(2,1)} %fusion.5) | data formatting | bytes 2097152 | tf_op jit(solution)/shard_map/dot_general | solution.py:64
  72.1 0.1 multiply_bitcast_fusion
  72.2 28.7 %all_to_all.20 = bf16[32,64,256]{2,1,0:T(8,128)(2,1)S(1)} all-to-all(bf16[32,64,256]{2,1,0:T(8,128)(2,1)S(1)} %multiply_bitcast_fusion), channel_id=1, replica_groups=mesh['feat'=32,'ex'=4] {'feat'}, dimensions={0} | all-to-all | bytes 2097152 | tf_op jit(solution)/shard_map/all_to_all | solution.py:74
  100.9 0.2 convert_reduce_fusion.1
  101.1 7.0 %all_to_all.21 = bf16[4,64,256]{2,1,0:T(8,128)(2,1)S(1)} all-to-all(bf16[4,64,256]{2,1,0:T(8,128)(2,1)S(1)} %broadcast_in_dim.5), channel_id=1, replica_groups=mesh['feat'=32,'ex'=4] {'ex'}, dimensions={0} | all-to-all | bytes 262144 | tf_op jit(solution)/shard_map/all_to_all | solution.py:79
  108.1 0.0 copy-done
  108.1 2.1 %fusion.8 = bf16[4,8,64,512]{3,2,1,0:T(8,128)(2,1)} fusion(bf16[8,512,256,1]{2,1,0,3:T(8,128)(2,1)S(1)} %bitcast.22, bf16[4,64,256]{2,1,0:T(8,128)(2,1)S(1)} %all_to_all.21), kind=kOutput, calls=%fused_computation.19 | convolution fusion | flops 538968064 | bytes 4325376 | tf_op jit(solution)/shard_map/dot_general | solution.py:82
  110.1 4.4 %all-to-all-start.2 = ((bf16[4,8,64,512]{3,2,1,0:T(8,128)(2,1)}), bf16[4,8,64,512]{3,2,1,0:T(8,128)(2,1)}, u32[]{:S(2)}, u32[]{:S(2)}) async-start(bf16[4,8,64,512]{3,2,1,0:T(8,128)(2,1)} %fusion.8), calls=%async_computation.2 | async-start | bytes 4194304 | tf_op jit(solution)/shard_map/all_to_all | solution.py:90
  114.6 0.0 copy-done.2
  114.6 25.7 %all-to-all-done.2 = bf16[4,8,64,512]{3,2,1,0:T(8,128)(2,1)} async-done(((bf16[4,8,64,512]{3,2,1,0:T(8,128)(2,1)}), bf16[4,8,64,512]{3,2,1,0:T(8,128)(2,1)}, u32[]{:S(2)}, u32[]{:S(2)}) %all-to-all-start.2) | async-done | bytes 2097184 | tf_op jit(solution)/shard_map/all_to_all | solution.py:90
  140.3 3.6 %gather_fusion = bf16[32,64,512]{2,1,0:T(8,128)(2,1)} fusion(bf16[32,64,512]{2,1,0:T(8,128)(2,1)} %bitcast.8, s32[1024]{0:T(1024)S(1)} %pad_clamp_fusion), kind=kCustom, calls=%fused_computation | custom fusion | bytes 4194432 | tf_op jit(solution)/shard_map/jit(_take)/gather | solution.py:91
  143.9 34.4 %all_to_all.22 = bf16[32,64,512]{2,1,0:T(8,128)(2,1)S(1)} all-to-all(bf16[32,64,512]{2,1,0:T(8,128)(2,1)} %gather_fusion), channel_id=1, replica_groups=mesh['feat'=32,'ex'=4] {'feat'}, dimensions={0} | all-to-all | bytes 4194304 | tf_op jit(solution)/shard_map/all_to_all | solution.py:92
  178.3 0.9 convert_reduce_fusion
  (7 shorter events, 0.1 us)
Async XLA Ops:
  0.0 108.1 %copy-start = (bf16[4096,256]{1,0:T(8,128)(2,1)S(1)}, bf16[4096,256]{1,0:T(8,128)(2,1)}, u32[]{:S(2)}) copy-start(bf16[4096,256]{1,0:T(8,128)(2,1)} %param.8) | copy-start | bytes 6291460
  18.6 14.0 %copy-start.1 = (s32[8192]{0:T(1024)S(1)}, s32[8192]{0:T(1024)}, u32[]{:S(2)}) copy-start(s32[8192]{0:T(1024)} %param.7) | copy-start | bytes 98308
  69.3 45.3 %copy-start.2 = (s32[32]{0:T(128)S(1)}, s32[32]{0:T(128)}, u32[]{:S(2)}) copy-start(s32[32]{0:T(128)} %param.9) | copy-start | bytes 388
  110.1 30.2 %all-to-all-start.2 = ((bf16[4,8,64,512]{3,2,1,0:T(8,128)(2,1)}), bf16[4,8,64,512]{3,2,1,0:T(8,128)(2,1)}, u32[]{:S(2)}, u32[]{:S(2)}) async-start(bf16[4,8,64,512]{3,2,1,0:T(8,128)(2,1)} %fusion.8), calls=%async_computation.2 | async-start | bytes 4194304 | tf_op jit(solution)/shard_map/all_to_all | solution.py:90
